TPU v7x, 512 devices: a whole 4x8x8 slice. The times are simulated.
512 devices in a mesh: wide: 32 (over z, x), narrow: 16 (over y, core).
Axes of the slice: x: 4, y: 8, z: 8, core: 2. Of those that a mesh axis runs over, the one named last changes fastest.
Arguments:
- a_blocks: bfloat16 [8192, 3, 128, 128], P(('wide', 'narrow')), may hold values from -6 to 6
- a_cols: int32 [8192, 3], P(('wide', 'narrow')), may hold values from 0 to 255, as said below
- prolong: bfloat16 [8192, 128, 128], P(('wide', 'narrow')), may hold values from -0.5 to 0.5
- owners: int32 [8192], P(('wide', 'narrow')), may hold values from 0 to 31, as said below
- slots: int32 [8192, 3], P(('wide', 'narrow')), may hold values from 0 to 23
Outputs:
- coarse: float32 [12288, 128, 128], P(('wide', 'narrow'))
Inputs may be any that keep to these rules, and one draw needn't show every extreme that they name: `a_cols`: the first entry of every block row is the block row itself (n * 16 + r). The other entries of one device's block rows name fine block rows of any one device of its narrow group at most 8 times, and in every narrow group one device is named exactly 8 times by every device of the group. `owners`: the block rows of one device name one owner at most 2 times; for every narrow index, one owner is named exactly 2 times by every device with that narrow index.
All inputs are finite; a program needn't handle non-finite values.
Results may differ from a plain program's by a relative error of at most 0.0041.
Values may be sent and summed in bfloat16 or wider, within the bound.
No kernel may reach another device: no remote copies, remote signals or barrier semaphores. Data moves between devices by JAX's collectives and lax.ppermute only.
A program may use at most 64 MiB of HBM per device.

v0:
```python
import jax
import jax.numpy as jnp
from jax import lax
from jax.sharding import PartitionSpec as P

CAP_OWNER = 2
CB_DEV = 24


def per_device(a_blocks, a_cols, prolong, owners, slots):
    slab_rows, per_row, block_size, unused_size = a_blocks.shape
    owner_count = lax.axis_size("wide")
    flat_cols = a_cols.reshape(-1)
    empty_blocks = jnp.zeros((slab_rows * per_row, block_size, block_size), jnp.bfloat16)
    shard_blocks = lax.all_gather(prolong, "narrow", axis=0, tiled=True)
    offset = jnp.int32(0)
    piece_rows = shard_blocks.shape[0]
    local_index = jnp.clip(flat_cols, 0, piece_rows - 1)
    inside = (flat_cols >= offset) & (flat_cols < offset + piece_rows)
    picked = jnp.take(shard_blocks, local_index, axis=0)
    right_blocks = jnp.where(inside[:, None, None], picked, empty_blocks)
    flat_a = a_blocks.reshape(slab_rows * per_row, block_size, block_size)
    product = jnp.einsum(
        "xij,xjl->xil", flat_a, right_blocks, preferred_element_type=jnp.float32
    ).astype(jnp.bfloat16)
    product = product.reshape(slab_rows, per_row, block_size, block_size)
    galerkin = jnp.einsum(
        "rji,rkjl->rkil", prolong, product, preferred_element_type=jnp.float32
    ).astype(jnp.bfloat16)
    row_ids = jnp.arange(slab_rows, dtype=jnp.int32)
    same_owner = (owners[:, None] == owners[None, :]) & (row_ids[None, :] < row_ids[:, None])
    owner_position = jnp.sum(same_owner.astype(jnp.int32), axis=1)
    bucket = owners * CAP_OWNER + owner_position
    bucket_map = jnp.arange(owner_count * CAP_OWNER, dtype=jnp.int32)[:, None] == bucket[None, :]
    outgoing = jnp.dot(
        bucket_map.astype(jnp.bfloat16),
        galerkin.reshape(slab_rows, per_row * block_size * block_size),
        preferred_element_type=jnp.float32,
    )
    outgoing = outgoing.astype(jnp.bfloat16).reshape(
        owner_count, CAP_OWNER * per_row, block_size, block_size
    )
    outgoing_slots = (
        jnp.sum(jnp.where(bucket_map[:, :, None], slots[None, :, :] + 1, 0), axis=1) - 1
    )
    outgoing_slots = outgoing_slots.reshape(owner_count, CAP_OWNER * per_row)
    arrived, arrived_slots = (
        lax.all_to_all(outgoing, "wide", split_axis=0, concat_axis=0, tiled=True),
        lax.all_to_all(outgoing_slots, "wide", split_axis=0, concat_axis=0, tiled=True),
    )
    target = jnp.arange(CB_DEV, dtype=jnp.int32)[:, None] == arrived_slots.reshape(-1)[None, :]
    coarse_sum = jnp.dot(
        target.astype(jnp.bfloat16),
        arrived.reshape(-1, block_size * block_size),
        preferred_element_type=jnp.float32,
    )
    return coarse_sum.reshape(CB_DEV, block_size, block_size)


def solution(mesh):
    return jax.shard_map(
        per_device,
        mesh=mesh,
        in_specs=(
            P(("wide", "narrow"), None, None, None),
            P(("wide", "narrow"), None),
            P(("wide", "narrow"), None, None),
            P(("wide", "narrow")),
            P(("wide", "narrow"), None),
        ),
        out_specs=P(("wide", "narrow"), None, None),
        check_vma=False,
    )
```

profile of v0, /device:TPU:7, one launch (start us, length us, event | category | flops | bytes accessed | tf_op | source)
XLA Modules:
  0.0 264.7 jit_solution(8379147805740310701)
XLA Ops:
  6.5 0.7 all-gather.2.cloned.1.call-update
  7.3 0.9 convert_reduce_fusion
  8.2 0.7 multiply_add_fusion
  8.9 0.7 broadcast_add_fusion.1
  9.7 0.1 copy.29
  9.8 0.7 sub.7
  10.5 12.8 %all-to-all-start = ((s32[32,1,6]{2,1,0:T(1,128)}), s32[32,1,6]{2,1,0:T(1,128)S(1)}, u32[]{:S(2)}, u32[]{:S(2)}) async-start(s32[32,1,6]{2,1,0:T(1,128)} %bitcast), calls=%async_computation | async-start | bytes 32768 | tf_op jit(solution)/shard_map/all_to_all | solution.py:49
  23.3 0.7 broadcast_clamp_fusion
  24.3 0.7 compare_and_fusion.1
  25.0 0.1 copy.31
  25.2 47.4 %all-gather.2.cloned.1.call-done = bf16[256,128,128]{2,1,0:T(8,128)(2,1)} async-done(((bf16[16,128,128]{2,1,0:T(8,128)(2,1)}), bf16[256,128,128]{2,1,0:T(8,128)(2,1)}) %all-gather.2.cloned.1.call-update) | async-done | bytes 8388624 | tf_op jit(solution)/shard_map/all_gather | solution.py:15
  72.6 4.2 %gather_fusion = bf16[48,128,128]{2,1,0:T(8,128)(2,1)S(1)} fusion(bf16[256,128,128]{2,1,0:T(8,128)(2,1)} %all-gather.2.cloned.1.call-done, s32[1024]{0:T(1024)S(1)} %pad_clamp_fusion), kind=kCustom, calls=%fused_computation | custom fusion | bytes 3145920 | tf_op jit(solution)/shard_map/jit(_take)/gather | solution.py:20
  76.9 1.4 convolution_convert_fusion.2
  78.3 0.6 fusion.9
  78.9 1.6 copy.35
  80.5 6.0 %convolution_convert_fusion = bf16[64,49152]{1,0:T(8,128)(2,1)} fusion(bf16[2,8,384,128]{3,2,1,0:T(8,128)(2,1)} %bitcast.39, s32[16]{0:T(128)S(1)} %multiply_add_fusion), kind=kOutput, calls=%fused_computation.1 | convolution fusion | flops 103810048 | bytes 7864384 | tf_op jit(solution)/shard_map/dot_general | solution.py:35
  86.4 9.0 %reshape.107 = bf16[32,6,128,128]{3,2,1,0:T(8,128)(2,1)} reshape(bf16[64,49152]{1,0:T(8,128)(2,1)} %convolution_convert_fusion) | data formatting | bytes 12582912 | tf_op jit(solution)/shard_map/reshape | solution.py:40
  95.4 10.0 %all-to-all-start.1 = ((bf16[32,6,128,128]{3,2,1,0:T(8,128)(2,1)}), bf16[32,6,128,128]{3,2,1,0:T(8,128)(2,1)}, u32[]{:S(2)}, u32[]{:S(2)}) async-start(bf16[32,6,128,128]{3,2,1,0:T(8,128)(2,1)} %reshape.107), calls=%async_computation.1 | async-start | bytes 12582912 | tf_op jit(solution)/shard_map/all_to_all | solution.py:48
  105.4 0.5 broadcast.102
  105.9 0.7 reduce.3
  106.6 0.1 eq.52
  106.7 143.5 %all-to-all-done.1 = bf16[32,6,128,128]{3,2,1,0:T(8,128)(2,1)} async-done(((bf16[32,6,128,128]{3,2,1,0:T(8,128)(2,1)}), bf16[32,6,128,128]{3,2,1,0:T(8,128)(2,1)}, u32[]{:S(2)}, u32[]{:S(2)}) %all-to-all-start.1) | async-done | bytes 6291488 | tf_op jit(solution)/shard_map/all_to_all | solution.py:48
  250.3 6.2 %fusion = f32[24,128,128]{2,0,1:T(8,128)S(1)} fusion(s32[192]{0:T(256)S(1)} %eq.52, bf16[24,8,128,128]{3,2,1,0:T(8,128)(2,1)} %bitcast.18), kind=kOutput, calls=%fused_computation.3 | convolution fusion | flops 150999552 | bytes 7865088 | tf_op jit(solution)/shard_map/dot_general | solution.py:52
  256.5 1.4 copy.37
  (16 shorter events, 0.6 us)
Async XLA Ops:
  6.5 70.3 %copy-start = (bf16[16,3,128,128]{3,2,1,0:T(8,128)(2,1)S(1)}, bf16[16,3,128,128]{3,2,1,0:T(8,128)(2,1)}, u32[]{:S(2)}) copy-start(bf16[16,3,128,128]{3,2,1,0:T(8,128)(2,1)} %param.5) | copy-start | bytes 4718596
  6.5 66.1 %all-gather.2.cloned.1.call-start = ((), (), s32[]{:S(2)}) async-start(), calls=%async_computation.2 | async-start | bytes 8912896 | tf_op jit(solution)/shard_map/all_gather | solution.py:15
  10.5 85.0 %all-to-all-start = ((s32[32,1,6]{2,1,0:T(1,128)}), s32[32,1,6]{2,1,0:T(1,128)S(1)}, u32[]{:S(2)}, u32[]{:S(2)}) async-start(s32[32,1,6]{2,1,0:T(1,128)} %bitcast), calls=%async_computation | async-start | bytes 32768 | tf_op jit(solution)/shard_map/all_to_all | solution.py:49
  76.9 1.4 copy-start.1
  95.4 154.8 %all-to-all-start.1 = ((bf16[32,6,128,128]{3,2,1,0:T(8,128)(2,1)}), bf16[32,6,128,128]{3,2,1,0:T(8,128)(2,1)}, u32[]{:S(2)}, u32[]{:S(2)}) async-start(bf16[32,6,128,128]{3,2,1,0:T(8,128)(2,1)} %reshape.107), calls=%async_computation.1 | async-start | bytes 12582912 | tf_op jit(solution)/shard_map/all_to_all | solution.py:48
Sparse Core Ops, SparseCore 0:
  9.5 63.1 all-gather.1
where the time goes:
time: 265 us
  waiting for transfers between devices  192 us (72%)
  starting transfers between devices  22.8 us (9%)
  local copies, waits for them, and re-layouts  18.1 us (7%)
  matrix products  14.2 us (5%)
  between operations  13.5 us (5%)
  other arithmetic  4.52 us (2%)
    all_to_all x1, waiting for transfers between devices, per_device(): lax.all_to_all(outgoing, 'wide', split_axis=0, concat_axis=0, tiled=True)  144 us
    all_gather x1, waiting for transfers between devices, per_device(): shard_blocks = lax.all_gather(prolong, 'narrow', axis=0, tiled=True)  47.4 us
    all_to_all x1, starting transfers between devices, per_device(): lax.all_to_all(outgoing_slots, 'wide', split_axis=0, concat_axis=0, tiled...  12.8 us
    all_to_all x1, starting transfers between devices, per_device(): lax.all_to_all(outgoing, 'wide', split_axis=0, concat_axis=0, tiled=True)  9.98 us
    reshape x1, local copies, waits for them, and re-layouts, per_device(): outgoing.astype(jnp.bfloat16)  9 us
    dot_general x1, matrix products, per_device(): jnp.dot(target.astype(jnp.bfloat16), arrived.reshape(-1, block_size * blo...  6.21 us
    dot_general x1, matrix products, per_device(): jnp.dot(bucket_map.astype(jnp.bfloat16), galerkin.reshape(slab_rows, per_...  5.98 us
  transfers between devices with their start and end apart: 3, of which 2 were waited for; matrix products, arithmetic and copies ran while one was open for 11% of the time, Pallas kernels for 0%

commit v1 on v0

v1 whole, which is shorter than its diff:
```python
import jax
import jax.numpy as jnp
from jax import lax
from jax.sharding import PartitionSpec as P

CAP_OWNER = 2
CB_DEV = 24


def galerkin_of(left, right, prolong_rows):
    product = jnp.einsum(
        "rkij,rkjl->rkil", left, right, preferred_element_type=jnp.float32
    ).astype(jnp.bfloat16)
    return jnp.einsum(
        "rji,rkjl->rkil", prolong_rows, product, preferred_element_type=jnp.float32
    ).astype(jnp.bfloat16)


def bucket_blocks(bucket_map, galerkin, owner_count):
    slab_rows, per_row, block_size, unused_size = galerkin.shape
    outgoing = jnp.dot(
        bucket_map.astype(jnp.bfloat16),
        galerkin.reshape(slab_rows, per_row * block_size * block_size),
        preferred_element_type=jnp.float32,
    )
    return outgoing.astype(jnp.bfloat16).reshape(
        owner_count, CAP_OWNER * per_row, block_size, block_size
    )


def per_device(a_blocks, a_cols, prolong, owners, slots):
    slab_rows, per_row, block_size, unused_size = a_blocks.shape
    owner_count = lax.axis_size("wide")

    row_ids = jnp.arange(slab_rows, dtype=jnp.int32)
    same_owner = (owners[:, None] == owners[None, :]) & (row_ids[None, :] < row_ids[:, None])
    owner_position = jnp.sum(same_owner.astype(jnp.int32), axis=1)
    bucket = owners * CAP_OWNER + owner_position
    bucket_map = jnp.arange(owner_count * CAP_OWNER, dtype=jnp.int32)[:, None] == bucket[None, :]
    outgoing_slots = (
        jnp.sum(jnp.where(bucket_map[:, :, None], slots[None, :, :] + 1, 0), axis=1) - 1
    )
    outgoing_slots = outgoing_slots.reshape(owner_count, CAP_OWNER, per_row)
    arrived_slots = lax.all_to_all(outgoing_slots, "wide", split_axis=0, concat_axis=0, tiled=True)

    galerkin_diag = galerkin_of(a_blocks[:, :1], prolong[:, None], prolong)
    outgoing_diag = bucket_blocks(bucket_map, galerkin_diag, owner_count)
    arrived_diag = lax.all_to_all(outgoing_diag, "wide", split_axis=0, concat_axis=0, tiled=True)

    shard_blocks = lax.all_gather(prolong, "narrow", axis=0, tiled=True)
    piece_rows = shard_blocks.shape[0]
    off_cols = jnp.clip(a_cols[:, 1:].reshape(-1), 0, piece_rows - 1)
    right_blocks = jnp.take(shard_blocks, off_cols, axis=0).reshape(
        slab_rows, per_row - 1, block_size, block_size
    )
    galerkin_off = galerkin_of(a_blocks[:, 1:], right_blocks, prolong)
    outgoing_off = bucket_blocks(bucket_map, galerkin_off, owner_count)
    arrived_off = lax.all_to_all(outgoing_off, "wide", split_axis=0, concat_axis=0, tiled=True)

    slots_diag = arrived_slots[:, :, :1].reshape(-1)
    slots_off = arrived_slots[:, :, 1:].reshape(-1)
    slot_ids = jnp.arange(CB_DEV, dtype=jnp.int32)[:, None]
    coarse_sum = jnp.dot(
        (slot_ids == slots_diag[None, :]).astype(jnp.bfloat16),
        arrived_diag.reshape(-1, block_size * block_size),
        preferred_element_type=jnp.float32,
    ) + jnp.dot(
        (slot_ids == slots_off[None, :]).astype(jnp.bfloat16),
        arrived_off.reshape(-1, block_size * block_size),
        preferred_element_type=jnp.float32,
    )
    return coarse_sum.reshape(CB_DEV, block_size, block_size)


def solution(mesh):
    return jax.shard_map(
        per_device,
        mesh=mesh,
        in_specs=(
            P(("wide", "narrow"), None, None, None),
            P(("wide", "narrow"), None),
            P(("wide", "narrow"), None, None),
            P(("wide", "narrow")),
            P(("wide", "narrow"), None),
        ),
        out_specs=P(("wide", "narrow"), None, None),
        check_vma=False,
    )
```

time: 265 us -> 218 us (0.82); the launches traced: 265 us -> 214 us
  waiting for transfers between devices: 192 us -> 129 us
  starting transfers between devices: 22.8 us -> 29.9 us
  local copies, waits for them, and re-layouts: 18.1 us -> 21.9 us
  matrix products: 14.2 us -> 17.2 us
    all_to_all x1 -> x2, waiting for transfers between devices: 144 us -> 91.1 us  [the longest x1 91.1 us: per_device(): lax.all_to_all(outgoing_off, 'wide', split_axis=0, concat_axis=0, tiled=T...]
    all_gather x1, waiting for transfers between devices: 47.4 us -> 34.7 us  [per_device(): shard_blocks = lax.all_gather(prolong, 'narrow', axis=0, tiled=True)]
    all_to_all x1 -> x2, starting transfers between devices: 9.98 us -> 17 us  [the longest x1 9.98 us: per_device(): lax.all_to_all(outgoing_off, 'wide', split_axis=0, concat_axis=0, tiled=T...]
    unnamed x4 -> x6, local copies, waits for them, and re-layouts: 0.01 us -> 3.38 us
    gather x1 -> x2, local copies, waits for them, and re-layouts: 4.23 us -> 7.29 us  [per_device(): jnp.take(shard_blocks, off_cols, axis=0)]
    dot_general x4 -> x6, matrix products: 14.2 us -> 17.2 us  [the longest x2 5.57 us: galerkin_of(): jnp.einsum('rji,rkjl->rkil', prolong_rows, product, preferred_element_typ...]
  transfers between devices with their start and end apart: 3 -> 4, of which waited for: 2 -> 3; matrix products, arithmetic and copies ran while one was open for 11% -> 16% of each run, Pallas kernels for 0% -> 0%
where the time goes in v1:
time: 218 us; the launch traced here: 214 us
  waiting for transfers between devices  129 us (59%)
  starting transfers between devices  29.9 us (14%)
  local copies, waits for them, and re-layouts  21.9 us (10%)
  matrix products  17.2 us (8%)
  between operations  13.5 us (6%)
  other arithmetic  2.46 us (1%)
    all_to_all x1, waiting for transfers between devices, per_device(): lax.all_to_all(outgoing_off, 'wide', split_axis=0, concat_axis=0, tiled=T...  91.1 us
    all_gather x1, waiting for transfers between devices, per_device(): shard_blocks = lax.all_gather(prolong, 'narrow', axis=0, tiled=True)  34.7 us
    all_to_all x1, starting transfers between devices, per_device(): lax.all_to_all(outgoing_slots, 'wide', split_axis=0, concat_axis=0, tiled...  12.8 us
    all_to_all x1, starting transfers between devices, per_device(): lax.all_to_all(outgoing_off, 'wide', split_axis=0, concat_axis=0, tiled=T...  9.98 us
    reshape x1, local copies, waits for them, and re-layouts, bucket_blocks(): outgoing.astype(jnp.bfloat16)  7.38 us
    gather x2, local copies, waits for them, and re-layouts, per_device(): jnp.take(shard_blocks, off_cols, axis=0)  7.29 us
    all_to_all x1, starting transfers between devices, per_device(): lax.all_to_all(outgoing_diag, 'wide', split_axis=0, concat_axis=0, tiled=...  7.02 us
    dot_general x2, matrix products, galerkin_of(): jnp.einsum('rji,rkjl->rkil', prolong_rows, product, preferred_element_typ...  5.57 us
  transfers between devices with their start and end apart: 4, of which 3 were waited for; matrix products, arithmetic and copies ran while one was open for 16% of the time, Pallas kernels for 0%

profile of v1, /device:TPU:7, one launch (start us, length us, event | category | flops | bytes accessed | tf_op | source)
XLA Modules:
  0.0 213.8 jit_solution(1906529896154253238)
XLA Ops:
  6.5 0.7 all-gather.2.cloned.1.call-update
  7.3 0.9 convert_reduce_fusion
  8.2 0.7 multiply_add_fusion
  8.9 0.7 broadcast_add_fusion.1
  9.7 0.7 copy.48
  10.4 12.8 %all-to-all-start = ((s32[32,2,3]{2,1,0:T(2,128)}), s32[32,2,3]{2,1,0:T(2,128)S(1)}, u32[]{:S(2)}, u32[]{:S(2)}) async-start(s32[32,2,3]{2,1,0:T(2,128)} %bitcast), calls=%async_computation | async-start | bytes 65536 | tf_op jit(solution)/shard_map/all_to_all | solution.py:44
  23.3 1.9 fusion.11
  25.4 0.8 fusion.5
  26.3 2.0 copy.51
  28.2 2.3 %all-to-all-done = s32[32,2,3]{2,1,0:T(2,128)S(1)} async-done(((s32[32,2,3]{2,1,0:T(2,128)}), s32[32,2,3]{2,1,0:T(2,128)S(1)}, u32[]{:S(2)}, u32[]{:S(2)}) %all-to-all-start) | async-done | bytes 800 | tf_op jit(solution)/shard_map/all_to_all | solution.py:44
  30.6 7.0 %all-to-all-start.1 = ((bf16[32,2,128,128]{3,2,1,0:T(8,128)(2,1)}), bf16[32,2,128,128]{3,2,1,0:T(8,128)(2,1)S(1)}, u32[]{:S(2)}, u32[]{:S(2)}) async-start(bf16[32,2,128,128]{3,2,1,0:T(8,128)(2,1)} %bitcast.60), calls=%async_computation.1 | async-start | bytes 4194304 | tf_op jit(solution)/shard_map/all_to_all | solution.py:48
  37.9 34.7 %all-gather.2.cloned.1.call-done = bf16[256,128,128]{2,1,0:T(8,128)(2,1)} async-done(((bf16[16,128,128]{2,1,0:T(8,128)(2,1)}), bf16[256,128,128]{2,1,0:T(8,128)(2,1)}) %all-gather.2.cloned.1.call-update) | async-done | bytes 8388624 | tf_op jit(solution)/shard_map/all_gather | solution.py:50
  72.6 5.0 %gather_fusion = bf16[32,128,128]{2,1,0:T(8,128)(2,1)} fusion(bf16[256,128,128]{2,1,0:T(8,128)(2,1)} %all-gather.2.cloned.1.call-done, s32[1024]{0:T(1024)S(1)} %pad_clamp_fusion), kind=kCustom, calls=%fused_computation | custom fusion | bytes 2097280 | tf_op jit(solution)/shard_map/jit(_take)/gather | solution.py:53
  77.7 2.3 %copy.44 = bf16[16,2,128,128]{2,3,1,0:T(8,128)(2,1)} copy(bf16[16,2,128,128]{3,2,1,0:T(8,128)(2,1)} %bitcast.61) | data formatting | bytes 2097152 | tf_op jit(solution)/shard_map/jit(_take)/gather | solution.py:53
  79.9 3.7 %fusion.10 = bf16[16,2,128,128]{2,3,1,0:T(8,128)(2,1)} fusion(bf16[16,3,128,128]{3,2,1,0:T(8,128)(2,1)} %param.5, bf16[16,2,128,128]{2,3,1,0:T(8,128)(2,1)} %copy.44, pred[16,2]{1,0:T(8,128)(4,1)S(1)} %copy.42, bf16[16,128,128]{2,1,0:T(8,128)(2,1)S(1)} %copy-done), kind=kOutput, calls=%fused_computation.14 | convolution fusion | flops 270008320 | bytes 3670048 | tf_op jit(solution)/shard_map/rji,rkjl->rkil/dot_general | solution.py:14
  83.6 1.6 copy.45
  85.3 3.3 %convolution_convert_fusion = bf16[64,32768]{1,0:T(8,128)(2,1)} fusion(bf16[2,8,256,128]{3,2,1,0:T(8,128)(2,1)S(1)} %bitcast.62, s32[16]{0:T(128)S(1)} %multiply_add_fusion), kind=kOutput, calls=%fused_computation.1 | convolution fusion | flops 69207040 | bytes 5242944 | tf_op jit(solution)/shard_map/dot_general | solution.py:21
  88.6 7.4 %reshape.97 = bf16[32,4,128,128]{3,2,1,0:T(8,128)(2,1)} reshape(bf16[64,32768]{1,0:T(8,128)(2,1)} %convolution_convert_fusion) | data formatting | bytes 8388608 | tf_op jit(solution)/shard_map/reshape | solution.py:26
  96.0 10.0 %all-to-all-start.2 = ((bf16[32,4,128,128]{3,2,1,0:T(8,128)(2,1)}), bf16[32,4,128,128]{3,2,1,0:T(8,128)(2,1)}, u32[]{:S(2)}, u32[]{:S(2)}) async-start(bf16[32,4,128,128]{3,2,1,0:T(8,128)(2,1)} %reshape.97), calls=%async_computation.2 | async-start | bytes 8388608 | tf_op jit(solution)/shard_map/all_to_all | solution.py:58
  106.0 0.6 slice_reduce_fusion
  106.9 2.4 %fusion.2 = f32[24,16384]{1,0:T(8,128)} fusion(bf16[8,8,128,128]{3,2,1,0:T(8,128)(2,1)S(1)} %bitcast.59, s32[64]{0:T(128)S(1)} %eq.67), kind=kOutput, calls=%fused_computation.6 | convolution fusion | flops 50333184 | bytes 3670272 | tf_op jit(solution)/shard_map/dot_general | solution.py:63
  109.3 91.1 %all-to-all-done.2 = bf16[32,4,128,128]{3,2,1,0:T(8,128)(2,1)} async-done(((bf16[32,4,128,128]{3,2,1,0:T(8,128)(2,1)}), bf16[32,4,128,128]{3,2,1,0:T(8,128)(2,1)}, u32[]{:S(2)}, u32[]{:S(2)}) %all-to-all-start.2) | async-done | bytes 4194336 | tf_op jit(solution)/shard_map/all_to_all | solution.py:58
  200.4 5.1 %fusion.6 = f32[3,8,128,128]{3,1,2,0:T(8,128)S(1)} fusion(f32[24,16384]{1,0:T(8,128)} %fusion.2, bf16[16,8,128,128]{3,2,1,0:T(8,128)(2,1)} %bitcast.28, s32[128]{0:T(128)S(1)} %eq.71), kind=kOutput, calls=%fused_computation.10 | convolution fusion | flops 101059584 | bytes 7340544 | tf_op jit(solution)/shard_map/dot_general | solution.py:67
  205.5 1.4 copy.55
  (20 shorter events, 1.1 us)
Async XLA Ops:
  6.5 66.1 %all-gather.2.cloned.1.call-start = ((), (), s32[]{:S(2)}) async-start(), calls=%async_computation.3 | async-start | bytes 8912896 | tf_op jit(solution)/shard_map/all_gather | solution.py:50
  10.4 20.1 %all-to-all-start = ((s32[32,2,3]{2,1,0:T(2,128)}), s32[32,2,3]{2,1,0:T(2,128)S(1)}, u32[]{:S(2)}, u32[]{:S(2)}) async-start(s32[32,2,3]{2,1,0:T(2,128)} %bitcast), calls=%async_computation | async-start | bytes 65536 | tf_op jit(solution)/shard_map/all_to_all | solution.py:44
  30.6 7.0 %copy-start.1 = (s32[16,3]{0,1:T(4,128)S(1)}, s32[16,3]{0,1:T(4,128)}, u32[]{:S(2)}) copy-start(s32[16,3]{0,1:T(4,128)} %param.6) | copy-start | bytes 580
  30.6 65.4 %all-to-all-start.1 = ((bf16[32,2,128,128]{3,2,1,0:T(8,128)(2,1)}), bf16[32,2,128,128]{3,2,1,0:T(8,128)(2,1)S(1)}, u32[]{:S(2)}, u32[]{:S(2)}) async-start(bf16[32,2,128,128]{3,2,1,0:T(8,128)(2,1)} %bitcast.60), calls=%async_computation.1 | async-start | bytes 4194304 | tf_op jit(solution)/shard_map/all_to_all | solution.py:48
  37.9 42.0 %copy-start = (bf16[16,128,128]{2,1,0:T(8,128)(2,1)S(1)}, bf16[16,128,128]{2,1,0:T(8,128)(2,1)}, u32[]{:S(2)}) copy-start(bf16[16,128,128]{2,1,0:T(8,128)(2,1)} %param.7) | copy-start | bytes 1572868
  96.0 104.5 %all-to-all-start.2 = ((bf16[32,4,128,128]{3,2,1,0:T(8,128)(2,1)}), bf16[32,4,128,128]{3,2,1,0:T(8,128)(2,1)}, u32[]{:S(2)}, u32[]{:S(2)}) async-start(bf16[32,4,128,128]{3,2,1,0:T(8,128)(2,1)} %reshape.97), calls=%async_computation.2 | async-start | bytes 8388608 | tf_op jit(solution)/shard_map/all_to_all | solution.py:58
Sparse Core Ops, SparseCore 0:
  9.4 63.1 all-gather.1

commit v2 on v1

v2 whole, which is shorter than its diff:
```python
import functools

import jax
import jax.numpy as jnp
from jax import lax
from jax.experimental import pallas as pl
from jax.experimental.pallas import tpu as pltpu
from jax.sharding import PartitionSpec as P

CAP_OWNER = 2
CB_DEV = 24


def galerkin_kernel(n_k, bucket_ref, cols_ref, *refs):
    a_refs = refs[:n_k]
    right_refs = refs[n_k:2 * n_k]
    pt_ref = refs[2 * n_k]
    out_ref = refs[2 * n_k + 1]
    row = pl.program_id(0)

    @pl.when(row == 0)
    def _():
        out_ref[...] = jnp.zeros_like(out_ref)

    bucket = bucket_ref[row]
    for k in range(n_k):
        product = jnp.dot(
            a_refs[k][...], right_refs[k][...], preferred_element_type=jnp.float32
        ).astype(jnp.bfloat16)
        galerkin = jnp.dot(pt_ref[...], product, preferred_element_type=jnp.float32)
        out_ref[bucket, k] = galerkin.astype(jnp.bfloat16)


def galerkin_buckets(a_blocks, ks, table, cols, prolong_t, bucket, bucket_count):
    slab_rows, unused_k, block_size, unused_size = a_blocks.shape
    n_k = len(ks)
    squeezed = pl.Squeezed()
    a_specs = [
        pl.BlockSpec((squeezed, squeezed, block_size, block_size),
                     functools.partial(lambda k, r, b, c: (r, k, 0, 0), k))
        for k in ks
    ]
    right_specs = [
        pl.BlockSpec((squeezed, block_size, block_size),
                     functools.partial(lambda j, r, b, c: (c[r, j], 0, 0), j))
        for j in range(n_k)
    ]
    pt_spec = pl.BlockSpec((squeezed, block_size, block_size), lambda r, b, c: (r, 0, 0))
    out_spec = pl.BlockSpec(
        (bucket_count, n_k, block_size, block_size), lambda r, b, c: (0, 0, 0, 0)
    )
    flops = 4 * slab_rows * n_k * block_size ** 3
    moved = 2 * block_size * block_size * (slab_rows * (2 * n_k + 1) + bucket_count * n_k)
    return pl.pallas_call(
        functools.partial(galerkin_kernel, n_k),
        out_shape=jax.ShapeDtypeStruct((bucket_count, n_k, block_size, block_size), jnp.bfloat16),
        grid_spec=pltpu.PrefetchScalarGridSpec(
            num_scalar_prefetch=2,
            grid=(slab_rows,),
            in_specs=a_specs * 1 + right_specs + [pt_spec],
            out_specs=out_spec,
        ),
        compiler_params=pltpu.CompilerParams(dimension_semantics=("arbitrary",)),
        cost_estimate=pl.CostEstimate(flops=flops, bytes_accessed=moved, transcendentals=0),
    )(bucket, cols, *([a_blocks] * n_k), *([table] * n_k), prolong_t)


def per_device(a_blocks, a_cols, prolong, owners, slots):
    slab_rows, per_row, block_size, unused_size = a_blocks.shape
    owner_count = lax.axis_size("wide")
    bucket_count = owner_count * CAP_OWNER

    row_ids = jnp.arange(slab_rows, dtype=jnp.int32)
    same_owner = (owners[:, None] == owners[None, :]) & (row_ids[None, :] < row_ids[:, None])
    owner_position = jnp.sum(same_owner.astype(jnp.int32), axis=1)
    bucket = jnp.clip(owners * CAP_OWNER + owner_position, 0, bucket_count - 1).astype(jnp.int32)
    bucket_map = jnp.arange(bucket_count, dtype=jnp.int32)[:, None] == bucket[None, :]
    outgoing_slots = (
        jnp.sum(jnp.where(bucket_map[:, :, None], slots[None, :, :] + 1, 0), axis=1) - 1
    )
    outgoing_slots = outgoing_slots.reshape(owner_count, CAP_OWNER, per_row)
    arrived_slots = lax.all_to_all(outgoing_slots, "wide", split_axis=0, concat_axis=0, tiled=True)

    prolong_t = jnp.swapaxes(prolong, 1, 2)

    outgoing_diag = galerkin_buckets(
        a_blocks, (0,), prolong, row_ids[:, None], prolong_t, bucket, bucket_count
    ).reshape(owner_count, CAP_OWNER, block_size, block_size)
    arrived_diag = lax.all_to_all(outgoing_diag, "wide", split_axis=0, concat_axis=0, tiled=True)

    shard_blocks = lax.all_gather(prolong, "narrow", axis=0, tiled=True)
    piece_rows = shard_blocks.shape[0]
    off_cols = jnp.clip(a_cols[:, 1:], 0, piece_rows - 1).astype(jnp.int32)
    outgoing_off = galerkin_buckets(
        a_blocks, tuple(range(1, per_row)), shard_blocks, off_cols, prolong_t, bucket, bucket_count
    ).reshape(owner_count, CAP_OWNER * (per_row - 1), block_size, block_size)
    arrived_off = lax.all_to_all(outgoing_off, "wide", split_axis=0, concat_axis=0, tiled=True)

    slots_diag = arrived_slots[:, :, :1].reshape(-1)
    slots_off = arrived_slots[:, :, 1:].reshape(-1)
    slot_ids = jnp.arange(CB_DEV, dtype=jnp.int32)[:, None]
    coarse_sum = jnp.dot(
        (slot_ids == slots_diag[None, :]).astype(jnp.bfloat16),
        arrived_diag.reshape(-1, block_size * block_size),
        preferred_element_type=jnp.float32,
    ) + jnp.dot(
        (slot_ids == slots_off[None, :]).astype(jnp.bfloat16),
        arrived_off.reshape(-1, block_size * block_size),
        preferred_element_type=jnp.float32,
    )
    return coarse_sum.reshape(CB_DEV, block_size, block_size)


def solution(mesh):
    return jax.shard_map(
        per_device,
        mesh=mesh,
        in_specs=(
            P(("wide", "narrow"), None, None, None),
            P(("wide", "narrow"), None),
            P(("wide", "narrow"), None, None),
            P(("wide", "narrow")),
            P(("wide", "narrow"), None),
        ),
        out_specs=P(("wide", "narrow"), None, None),
        check_vma=False,
    )
```

time: 218 us -> 213 us (0.977)
  Pallas kernels: 0 us -> 24.3 us
  local copies, waits for them, and re-layouts: 21.9 us -> 5.83 us
  matrix products: 17.2 us -> 7.46 us
  starting transfers between devices: 29.9 us -> 27.1 us
    pallas_call x0 -> x2, Pallas kernels: none -> 24.3 us  [galerkin_buckets(): pl.pallas_call(functools.partial(galerkin_kernel, n_k), out_shape=jax.Sha...]
    all_to_all x1, waiting for transfers between devices: 0.01 us -> 11.1 us  [per_device(): lax.all_to_all(outgoing_diag, 'wide', split_axis=0, concat_axis=0, tiled=...]
    dot_general x4 -> x0, matrix products: 9.74 us -> none  [the longest x2 5.57 us: galerkin_of(): jnp.einsum('rji,rkjl->rkil', prolong_rows, product, preferred_element_typ...]
    all_gather x1, waiting for transfers between devices: 34.7 us -> 25.2 us  [per_device(): shard_blocks = lax.all_gather(prolong, 'narrow', axis=0, tiled=True)]
    reshape x1 -> x0, local copies, waits for them, and re-layouts: 7.38 us -> none  [bucket_blocks(): outgoing.astype(jnp.bfloat16)]
    gather x2 -> x0, local copies, waits for them, and re-layouts: 7.29 us -> none  [per_device(): jnp.take(shard_blocks, off_cols, axis=0)]
    all_to_all x1, starting transfers between devices: 9.98 us -> 4.88 us  [per_device(): lax.all_to_all(outgoing_off, 'wide', split_axis=0, concat_axis=0, tiled=T...]
    all_to_all x1, waiting for transfers between devices: 2.33 us -> 0.01 us  [per_device(): lax.all_to_all(outgoing_slots, 'wide', split_axis=0, concat_axis=0, tiled...]
  transfers between devices with their start and end apart: 4 -> 4, of which waited for: 3 -> 3; matrix products, arithmetic and copies ran while one was open for 16% -> 5% of each run, Pallas kernels for 0% -> 12%
where the time goes in v2:
time: 213 us; the launch traced here: 210 us
  waiting for transfers between devices  128 us (60%)
  starting transfers between devices  27.1 us (13%)
  Pallas kernels  24.3 us (11%)
  between operations  13.5 us (6%)
  matrix products  7.46 us (4%)
  local copies, waits for them, and re-layouts  5.83 us (3%)
  other arithmetic  3.03 us (1%)
    all_to_all x1, waiting for transfers between devices, per_device(): lax.all_to_all(outgoing_off, 'wide', split_axis=0, concat_axis=0, tiled=T...  91.4 us
    all_gather x1, waiting for transfers between devices, per_device(): shard_blocks = lax.all_gather(prolong, 'narrow', axis=0, tiled=True)  25.2 us
    pallas_call x2, Pallas kernels, galerkin_buckets(): pl.pallas_call(functools.partial(galerkin_kernel, n_k), out_shape=jax.Sha...  24.3 us
    all_to_all x1, starting transfers between devices, per_device(): lax.all_to_all(outgoing_slots, 'wide', split_axis=0, concat_axis=0, tiled...  12.8 us
    all_to_all x1, waiting for transfers between devices, per_device(): lax.all_to_all(outgoing_diag, 'wide', split_axis=0, concat_axis=0, tiled=...  11.1 us
    all_to_all x1, starting transfers between devices, per_device(): lax.all_to_all(outgoing_diag, 'wide', split_axis=0, concat_axis=0, tiled=...  9.34 us
    dot_general x1, matrix products, per_device(): jnp.dot((slot_ids == slots_off[None, :]).astype(jnp.bfloat16), arrived_of...  5.06 us
    all_to_all x1, starting transfers between devices, per_device(): lax.all_to_all(outgoing_off, 'wide', split_axis=0, concat_axis=0, tiled=T...  4.88 us
  transfers between devices with their start and end apart: 4, of which 3 were waited for; matrix products, arithmetic and copies ran while one was open for 5% of the time, Pallas kernels for 12%

profile of v2, /device:TPU:7, one launch (start us, length us, event | category | flops | bytes accessed | tf_op | source)
XLA Modules:
  0.0 209.6 jit_solution(8379762289598099434)
XLA Ops:
  6.5 0.7 all-gather.2.cloned.1.call-update
  7.3 0.9 convert_reduce_fusion
  8.2 0.7 add_clamp_fusion.bucket_ref
  8.9 0.7 broadcast_add_fusion.1
  9.6 0.1 select_reduce_fusion
  9.7 0.7 copy.24
  10.4 12.8 %all-to-all-start = ((s32[32,2,3]{2,1,0:T(2,128)}), s32[32,2,3]{2,1,0:T(2,128)S(1)}, u32[]{:S(2)}, u32[]{:S(2)}) async-start(s32[32,2,3]{2,1,0:T(2,128)} %bitcast), calls=%async_computation | async-start | bytes 65536 | tf_op jit(solution)/shard_map/all_to_all | solution.py:82
  23.3 2.0 copy.22
  25.3 0.6 iota.22.cols_ref
  25.9 11.5 %shard_map.55 = bf16[64,1,128,128]{3,2,1,0:T(8,128)(2,1)} custom-call(s32[16]{0:T(128)} %copy-done, s32[16,1]{1,0:T(8,128)} %iota.22.cols_ref, bf16[16,3,128,128]{3,2,1,0:T(8,128)(2,1)} %refs_1_.3, bf16[16,128,128]{2,1,0:T(8,128)(2,1)} %refs_1_.2, bf16[16,128,128]{2,1,0:T(8,128)(2,1)} %bitcast.22), custom_call_target="tpu_custom_call" | custom-call | flops 134217728 | bytes 3670016 | tf_op jit(solution)/shard_map/pallas_call | solution.py:54
  37.4 9.3 %all-to-all-start.1 = ((bf16[32,2,128,128]{3,2,1,0:T(8,128)(2,1)}), bf16[32,2,128,128]{3,2,1,0:T(8,128)(2,1)S(1)}, u32[]{:S(2)}, u32[]{:S(2)}) async-start(bf16[32,2,128,128]{3,2,1,0:T(8,128)(2,1)} %bitcast.20), calls=%async_computation.1 | async-start | bytes 4194304 | tf_op jit(solution)/shard_map/all_to_all | solution.py:89
  46.8 0.6 broadcast_clamp_fusion.cols_ref
  47.4 25.2 %all-gather.2.cloned.1.call-done.refs_2_.refs_3_ = bf16[256,128,128]{2,1,0:T(8,128)(2,1)} async-done(((bf16[16,128,128]{2,1,0:T(8,128)(2,1)}), bf16[256,128,128]{2,1,0:T(8,128)(2,1)}) %all-gather.2.cloned.1.call-update) | async-done | bytes 8388624 | tf_op jit(solution)/shard_map/all_gather | solution.py:91
  72.6 12.9 %shard_map.56 = bf16[64,2,128,128]{3,2,1,0:T(8,128)(2,1)} custom-call(s32[16]{0:T(128)} %copy-done, s32[16,2]{1,0:T(8,128)} %broadcast_clamp_fusion.cols_ref, bf16[16,3,128,128]{3,2,1,0:T(8,128)(2,1)} %refs_1_.3, bf16[16,3,128,128]{3,2,1,0:T(8,128)(2,1)} %refs_1_.3, bf16[256,128,128]{2,1,0:T(8,128)(2,1)} %all-gather.2.cloned.1.call-done.refs_2_.refs_3_, ...), custom_call_target="tpu_custom_call" | custom-call | flops 268435456 | bytes 6815744 | tf_op jit(solution)/shard_map/pallas_call | solution.py:54
  85.5 11.1 %all-to-all-done.1 = bf16[32,2,128,128]{3,2,1,0:T(8,128)(2,1)S(1)} async-done(((bf16[32,2,128,128]{3,2,1,0:T(8,128)(2,1)}), bf16[32,2,128,128]{3,2,1,0:T(8,128)(2,1)S(1)}, u32[]{:S(2)}, u32[]{:S(2)}) %all-to-all-start.1) | async-done | bytes 2097184 | tf_op jit(solution)/shard_map/all_to_all | solution.py:89
  96.6 4.9 %all-to-all-start.2 = ((bf16[32,4,128,128]{3,2,1,0:T(8,128)(2,1)}), bf16[32,4,128,128]{3,2,1,0:T(8,128)(2,1)}, u32[]{:S(2)}, u32[]{:S(2)}) async-start(bf16[32,4,128,128]{3,2,1,0:T(8,128)(2,1)} %bitcast.19), calls=%async_computation.2 | async-start | bytes 8388608 | tf_op jit(solution)/shard_map/all_to_all | solution.py:97
  101.5 0.6 slice_reduce_fusion
  102.1 0.1 eq.67
  102.2 0.1 slice.13
  102.3 0.2 eq.71
  102.4 2.4 %fusion.2 = f32[24,16384]{1,0:T(8,128)} fusion(bf16[8,8,128,128]{3,2,1,0:T(8,128)(2,1)S(1)} %bitcast.21, s32[64]{0:T(128)S(1)} %eq.67), kind=kOutput, calls=%fused_computation.3 | convolution fusion | flops 50333184 | bytes 3670272 | tf_op jit(solution)/shard_map/dot_general | solution.py:102
  104.8 91.4 %all-to-all-done.2 = bf16[32,4,128,128]{3,2,1,0:T(8,128)(2,1)} async-done(((bf16[32,4,128,128]{3,2,1,0:T(8,128)(2,1)}), bf16[32,4,128,128]{3,2,1,0:T(8,128)(2,1)}, u32[]{:S(2)}, u32[]{:S(2)}) %all-to-all-start.2) | async-done | bytes 4194336 | tf_op jit(solution)/shard_map/all_to_all | solution.py:97
  196.2 5.1 %fusion.5 = f32[3,8,128,128]{3,1,2,0:T(8,128)S(1)} fusion(f32[24,16384]{1,0:T(8,128)} %fusion.2, bf16[16,8,128,128]{3,2,1,0:T(8,128)(2,1)} %bitcast.8, s32[128]{0:T(128)S(1)} %eq.71), kind=kOutput, calls=%fused_computation.6 | convolution fusion | flops 101059584 | bytes 7340544 | tf_op jit(solution)/shard_map/dot_general | solution.py:106
  201.3 1.4 copy.28
  (10 shorter events, 0.2 us)
Async XLA Ops:
  6.5 66.1 %all-gather.2.cloned.1.call-start = ((), (), s32[]{:S(2)}) async-start(), calls=%async_computation.3 | async-start | bytes 8912896 | tf_op jit(solution)/shard_map/all_gather | solution.py:91
  8.8 17.1 %copy-start = (s32[16]{0:T(128)}, s32[16]{0:T(128)S(1)}, u32[]{:S(2)}) copy-start(s32[16]{0:T(128)S(1)} %add_clamp_fusion.bucket_ref) | copy-start | bytes 196
  10.4 27.0 %all-to-all-start = ((s32[32,2,3]{2,1,0:T(2,128)}), s32[32,2,3]{2,1,0:T(2,128)S(1)}, u32[]{:S(2)}, u32[]{:S(2)}) async-start(s32[32,2,3]{2,1,0:T(2,128)} %bitcast), calls=%async_computation | async-start | bytes 65536 | tf_op jit(solution)/shard_map/all_to_all | solution.py:82
  37.4 9.3 %copy-start.1 = (s32[16,3]{0,1:T(4,128)S(1)}, s32[16,3]{0,1:T(4,128)}, u32[]{:S(2)}) copy-start(s32[16,3]{0,1:T(4,128)} %param.6) | copy-start | bytes 580
  37.4 59.2 %all-to-all-start.1 = ((bf16[32,2,128,128]{3,2,1,0:T(8,128)(2,1)}), bf16[32,2,128,128]{3,2,1,0:T(8,128)(2,1)S(1)}, u32[]{:S(2)}, u32[]{:S(2)}) async-start(bf16[32,2,128,128]{3,2,1,0:T(8,128)(2,1)} %bitcast.20), calls=%async_computation.1 | async-start | bytes 4194304 | tf_op jit(solution)/shard_map/all_to_all | solution.py:89
  96.6 99.7 %all-to-all-start.2 = ((bf16[32,4,128,128]{3,2,1,0:T(8,128)(2,1)}), bf16[32,4,128,128]{3,2,1,0:T(8,128)(2,1)}, u32[]{:S(2)}, u32[]{:S(2)}) async-start(bf16[32,4,128,128]{3,2,1,0:T(8,128)(2,1)} %bitcast.19), calls=%async_computation.2 | async-start | bytes 8388608 | tf_op jit(solution)/shard_map/all_to_all | solution.py:97
Sparse Core Ops, SparseCore 0:
  9.4 63.1 all-gather.1

commit v3 on v2

--- a/solution.py
+++ b/solution.py
@@ -11,24 +11,28 @@
 CB_DEV = 24
 
 
+ROWS_PER_STEP = 4
+
+
 def galerkin_kernel(n_k, bucket_ref, cols_ref, *refs):
     a_refs = refs[:n_k]
-    right_refs = refs[n_k:2 * n_k]
-    pt_ref = refs[2 * n_k]
-    out_ref = refs[2 * n_k + 1]
-    row = pl.program_id(0)
+    right_refs = refs[n_k:n_k + ROWS_PER_STEP * n_k]
+    pt_ref = refs[n_k + ROWS_PER_STEP * n_k]
+    out_ref = refs[n_k + ROWS_PER_STEP * n_k + 1]
+    step = pl.program_id(0)
 
-    @pl.when(row == 0)
+    @pl.when(step == 0)
     def _():
         out_ref[...] = jnp.zeros_like(out_ref)
 
-    bucket = bucket_ref[row]
-    for k in range(n_k):
-        product = jnp.dot(
-            a_refs[k][...], right_refs[k][...], preferred_element_type=jnp.float32
-        ).astype(jnp.bfloat16)
-        galerkin = jnp.dot(pt_ref[...], product, preferred_element_type=jnp.float32)
-        out_ref[bucket, k] = galerkin.astype(jnp.bfloat16)
+    for i in range(ROWS_PER_STEP):
+        bucket = bucket_ref[step * ROWS_PER_STEP + i]
+        for k in range(n_k):
+            product = jnp.dot(
+                a_refs[k][i], right_refs[i * n_k + k][...], preferred_element_type=jnp.float32
+            ).astype(jnp.bfloat16)
+            galerkin = jnp.dot(pt_ref[i], product, preferred_element_type=jnp.float32)
+            out_ref[bucket, k] = galerkin.astype(jnp.bfloat16)
 
 
 def galerkin_buckets(a_blocks, ks, table, cols, prolong_t, bucket, bucket_count):
@@ -36,18 +40,19 @@
     n_k = len(ks)
     squeezed = pl.Squeezed()
     a_specs = [
-        pl.BlockSpec((squeezed, squeezed, block_size, block_size),
-                     functools.partial(lambda k, r, b, c: (r, k, 0, 0), k))
+        pl.BlockSpec((ROWS_PER_STEP, squeezed, block_size, block_size),
+                     functools.partial(lambda k, s, b, c: (s, k, 0, 0), k))
         for k in ks
     ]
     right_specs = [
         pl.BlockSpec((squeezed, block_size, block_size),
-                     functools.partial(lambda j, r, b, c: (c[r, j], 0, 0), j))
+                     functools.partial(lambda i, j, s, b, c: (c[s * ROWS_PER_STEP + i, j], 0, 0), i, j))
+        for i in range(ROWS_PER_STEP)
         for j in range(n_k)
     ]
-    pt_spec = pl.BlockSpec((squeezed, block_size, block_size), lambda r, b, c: (r, 0, 0))
+    pt_spec = pl.BlockSpec((ROWS_PER_STEP, block_size, block_size), lambda s, b, c: (s, 0, 0))
     out_spec = pl.BlockSpec(
-        (bucket_count, n_k, block_size, block_size), lambda r, b, c: (0, 0, 0, 0)
+        (bucket_count, n_k, block_size, block_size), lambda s, b, c: (0, 0, 0, 0)
     )
     flops = 4 * slab_rows * n_k * block_size ** 3
     moved = 2 * block_size * block_size * (slab_rows * (2 * n_k + 1) + bucket_count * n_k)
@@ -56,13 +61,13 @@
         out_shape=jax.ShapeDtypeStruct((bucket_count, n_k, block_size, block_size), jnp.bfloat16),
         grid_spec=pltpu.PrefetchScalarGridSpec(
             num_scalar_prefetch=2,
-            grid=(slab_rows,),
-            in_specs=a_specs * 1 + right_specs + [pt_spec],
+            grid=(slab_rows // ROWS_PER_STEP,),
+            in_specs=a_specs + right_specs + [pt_spec],
             out_specs=out_spec,
         ),
         compiler_params=pltpu.CompilerParams(dimension_semantics=("arbitrary",)),
         cost_estimate=pl.CostEstimate(flops=flops, bytes_accessed=moved, transcendentals=0),
-    )(bucket, cols, *([a_blocks] * n_k), *([table] * n_k), prolong_t)
+    )(bucket, cols, *([a_blocks] * n_k), *([table] * (ROWS_PER_STEP * n_k)), prolong_t)
 
 
 def per_device(a_blocks, a_cols, prolong, owners, slots):

time: 213 us -> 206 us (0.967)
  Pallas kernels: 24.3 us -> 12.8 us
  waiting for transfers between devices: 128 us -> 134 us
    pallas_call x2, Pallas kernels: 24.3 us -> 12.8 us  [galerkin_buckets(): pl.pallas_call(functools.partial(galerkin_kernel, n_k), out_shape=jax.Sha...]
    all_gather x1, waiting for transfers between devices: 25.2 us -> 31 us  [per_device(): shard_blocks = lax.all_gather(prolong, 'narrow', axis=0, tiled=True)]
  transfers between devices with their start and end apart: 4 -> 4, of which waited for: 3 -> 3; matrix products, arithmetic and copies ran while one was open for 5% -> 5% of each run, Pallas kernels for 12% -> 6%
where the time goes in v3:
time: 206 us; the launch traced here: 204 us
  waiting for transfers between devices  134 us (65%)
  starting transfers between devices  26.9 us (13%)
  between operations  13.5 us (7%)
  Pallas kernels  12.8 us (6%)
  matrix products  7.46 us (4%)
  local copies, waits for them, and re-layouts  5.83 us (3%)
  other arithmetic  3.03 us (1%)
    all_to_all x1, waiting for transfers between devices, per_device(): lax.all_to_all(outgoing_off, 'wide', split_axis=0, concat_axis=0, tiled=T...  91.4 us
    all_gather x1, waiting for transfers between devices, per_device(): shard_blocks = lax.all_gather(prolong, 'narrow', axis=0, tiled=True)  31 us
    all_to_all x1, starting transfers between devices, per_device(): lax.all_to_all(outgoing_slots, 'wide', split_axis=0, concat_axis=0, tiled...  12.8 us
    pallas_call x2, Pallas kernels, galerkin_buckets(): pl.pallas_call(functools.partial(galerkin_kernel, n_k), out_shape=jax.Sha...  12.8 us
    all_to_all x1, waiting for transfers between devices, per_device(): lax.all_to_all(outgoing_diag, 'wide', split_axis=0, concat_axis=0, tiled=...  11.1 us
    all_to_all x1, starting transfers between devices, per_device(): lax.all_to_all(outgoing_diag, 'wide', split_axis=0, concat_axis=0, tiled=...  9.3 us
    dot_general x1, matrix products, per_device(): jnp.dot((slot_ids == slots_off[None, :]).astype(jnp.bfloat16), arrived_of...  5.06 us
    all_to_all x1, starting transfers between devices, per_device(): lax.all_to_all(outgoing_off, 'wide', split_axis=0, concat_axis=0, tiled=T...  4.79 us
  transfers between devices with their start and end apart: 4, of which 3 were waited for; matrix products, arithmetic and copies ran while one was open for 5% of the time, Pallas kernels for 6%

profile of v3, /device:TPU:7, one launch (start us, length us, event | category | flops | bytes accessed | tf_op | source)
XLA Modules:
  0.0 203.7 jit_solution(5965763710352371774)
XLA Ops:
  6.5 0.7 all-gather.2.cloned.1.call-update
  7.3 0.9 convert_reduce_fusion
  8.2 0.7 add_clamp_fusion.bucket_ref
  8.9 0.7 broadcast_add_fusion.1
  9.6 0.1 select_reduce_fusion
  9.7 0.7 copy.24
  10.4 12.8 %all-to-all-start = ((s32[32,2,3]{2,1,0:T(2,128)}), s32[32,2,3]{2,1,0:T(2,128)S(1)}, u32[]{:S(2)}, u32[]{:S(2)}) async-start(s32[32,2,3]{2,1,0:T(2,128)} %bitcast), calls=%async_computation | async-start | bytes 65536 | tf_op jit(solution)/shard_map/all_to_all | solution.py:87
  23.3 2.0 %copy.22 = bf16[16,128,128]{1,2,0:T(8,128)(2,1)} copy(bf16[16,128,128]{2,1,0:T(8,128)(2,1)} %refs_4_.1) | data formatting | bytes 1048576 | tf_op args[2]
  25.3 0.6 iota.22.cols_ref
  25.9 5.7 %shard_map.55 = bf16[64,1,128,128]{3,2,1,0:T(8,128)(2,1)} custom-call(s32[16]{0:T(128)} %copy-done, s32[16,1]{1,0:T(8,128)} %iota.22.cols_ref, bf16[16,3,128,128]{3,2,1,0:T(8,128)(2,1)} %refs_1_.3, bf16[16,128,128]{2,1,0:T(8,128)(2,1)} %refs_4_.1, bf16[16,128,128]{2,1,0:T(8,128)(2,1)} %refs_4_.1, bf16[16,128,128]{2,1,0:T(8,128)(2,1)} %refs_4_.1, ...), custom_call_target="tpu_custom_call" | custom-call | flops 134217728 | bytes 3670016 | tf_op jit(solution)/shard_map/pallas_call | solution.py:59
  31.6 9.3 %all-to-all-start.1 = ((bf16[32,2,128,128]{3,2,1,0:T(8,128)(2,1)}), bf16[32,2,128,128]{3,2,1,0:T(8,128)(2,1)S(1)}, u32[]{:S(2)}, u32[]{:S(2)}) async-start(bf16[32,2,128,128]{3,2,1,0:T(8,128)(2,1)} %bitcast.21), calls=%async_computation.1 | async-start | bytes 4194304 | tf_op jit(solution)/shard_map/all_to_all | solution.py:94
  41.0 0.6 broadcast_clamp_fusion.cols_ref
  41.6 31.0 %all-gather.2.cloned.1.call-done.refs_2_.refs_3_.refs_4_.refs_5_.refs_6_.refs_7_.refs_8_.refs_9_ = bf16[256,128,128]{2,1,0:T(8,128)(2,1)} async-done(((bf16[16,128,128]{2,1,0:T(8,128)(2,1)}), bf16[256,128,128]{2,1,0:T(8,128)(2,1)}) %all-gather.2.cloned.1.call-update) | async-done | bytes 8388624 | tf_op jit(solution)/shard_map/all_gather | solution.py:96
  72.6 7.1 %shard_map.56 = bf16[64,2,128,128]{3,2,1,0:T(8,128)(2,1)} custom-call(s32[16]{0:T(128)} %copy-done, s32[16,2]{1,0:T(8,128)} %broadcast_clamp_fusion.cols_ref, bf16[16,3,128,128]{3,2,1,0:T(8,128)(2,1)} %refs_1_.3, bf16[16,3,128,128]{3,2,1,0:T(8,128)(2,1)} %refs_1_.3, ...), custom_call_target="tpu_custom_call" | custom-call | flops 268435456 | bytes 6815744 | tf_op jit(solution)/shard_map/pallas_call | solution.py:59
  79.8 11.1 %all-to-all-done.1 = bf16[32,2,128,128]{3,2,1,0:T(8,128)(2,1)S(1)} async-done(((bf16[32,2,128,128]{3,2,1,0:T(8,128)(2,1)}), bf16[32,2,128,128]{3,2,1,0:T(8,128)(2,1)S(1)}, u32[]{:S(2)}, u32[]{:S(2)}) %all-to-all-start.1) | async-done | bytes 2097184 | tf_op jit(solution)/shard_map/all_to_all | solution.py:94
  90.8 4.8 %all-to-all-start.2 = ((bf16[32,4,128,128]{3,2,1,0:T(8,128)(2,1)}), bf16[32,4,128,128]{3,2,1,0:T(8,128)(2,1)}, u32[]{:S(2)}, u32[]{:S(2)}) async-start(bf16[32,4,128,128]{3,2,1,0:T(8,128)(2,1)} %bitcast.19), calls=%async_computation.2 | async-start | bytes 8388608 | tf_op jit(solution)/shard_map/all_to_all | solution.py:102
  95.6 0.6 slice_reduce_fusion
  96.3 0.1 eq.67
  96.4 0.1 slice.13
  96.5 0.2 eq.71
  96.6 2.4 %fusion.2 = f32[24,16384]{1,0:T(8,128)} fusion(bf16[8,8,128,128]{3,2,1,0:T(8,128)(2,1)S(1)} %bitcast.20, s32[64]{0:T(128)S(1)} %eq.67), kind=kOutput, calls=%fused_computation.3 | convolution fusion | flops 50333184 | bytes 3670272 | tf_op jit(solution)/shard_map/dot_general | solution.py:107
  99.0 91.4 %all-to-all-done.2 = bf16[32,4,128,128]{3,2,1,0:T(8,128)(2,1)} async-done(((bf16[32,4,128,128]{3,2,1,0:T(8,128)(2,1)}), bf16[32,4,128,128]{3,2,1,0:T(8,128)(2,1)}, u32[]{:S(2)}, u32[]{:S(2)}) %all-to-all-start.2) | async-done | bytes 4194336 | tf_op jit(solution)/shard_map/all_to_all | solution.py:102
  190.4 5.1 %fusion.5 = f32[3,8,128,128]{3,1,2,0:T(8,128)S(1)} fusion(f32[24,16384]{1,0:T(8,128)} %fusion.2, bf16[16,8,128,128]{3,2,1,0:T(8,128)(2,1)} %bitcast.8, s32[128]{0:T(128)S(1)} %eq.71), kind=kOutput, calls=%fused_computation.6 | convolution fusion | flops 101059584 | bytes 7340544 | tf_op jit(solution)/shard_map/dot_general | solution.py:111
  195.5 1.4 copy.28
  (10 shorter events, 0.2 us)
Async XLA Ops:
  6.5 66.1 %all-gather.2.cloned.1.call-start = ((), (), s32[]{:S(2)}) async-start(), calls=%async_computation.3 | async-start | bytes 8912896 | tf_op jit(solution)/shard_map/all_gather | solution.py:96
  8.8 17.1 %copy-start = (s32[16]{0:T(128)}, s32[16]{0:T(128)S(1)}, u32[]{:S(2)}) copy-start(s32[16]{0:T(128)S(1)} %add_clamp_fusion.bucket_ref) | copy-start | bytes 196
  10.4 21.2 %all-to-all-start = ((s32[32,2,3]{2,1,0:T(2,128)}), s32[32,2,3]{2,1,0:T(2,128)S(1)}, u32[]{:S(2)}, u32[]{:S(2)}) async-start(s32[32,2,3]{2,1,0:T(2,128)} %bitcast), calls=%async_computation | async-start | bytes 65536 | tf_op jit(solution)/shard_map/all_to_all | solution.py:87
  31.6 9.3 %copy-start.1 = (s32[16,3]{0,1:T(4,128)S(1)}, s32[16,3]{0,1:T(4,128)}, u32[]{:S(2)}) copy-start(s32[16,3]{0,1:T(4,128)} %param.6) | copy-start | bytes 580
  31.6 59.3 %all-to-all-start.1 = ((bf16[32,2,128,128]{3,2,1,0:T(8,128)(2,1)}), bf16[32,2,128,128]{3,2,1,0:T(8,128)(2,1)S(1)}, u32[]{:S(2)}, u32[]{:S(2)}) async-start(bf16[32,2,128,128]{3,2,1,0:T(8,128)(2,1)} %bitcast.21), calls=%async_computation.1 | async-start | bytes 4194304 | tf_op jit(solution)/shard_map/all_to_all | solution.py:94
  90.8 99.6 %all-to-all-start.2 = ((bf16[32,4,128,128]{3,2,1,0:T(8,128)(2,1)}), bf16[32,4,128,128]{3,2,1,0:T(8,128)(2,1)}, u32[]{:S(2)}, u32[]{:S(2)}) async-start(bf16[32,4,128,128]{3,2,1,0:T(8,128)(2,1)} %bitcast.19), calls=%async_computation.2 | async-start | bytes 8388608 | tf_op jit(solution)/shard_map/all_to_all | solution.py:102
Sparse Core Ops, SparseCore 0:
  9.4 63.1 all-gather.1

commit v4 on v3

--- a/solution.py
+++ b/solution.py
@@ -31,11 +31,13 @@
             product = jnp.dot(
                 a_refs[k][i], right_refs[i * n_k + k][...], preferred_element_type=jnp.float32
             ).astype(jnp.bfloat16)
-            galerkin = jnp.dot(pt_ref[i], product, preferred_element_type=jnp.float32)
+            galerkin = lax.dot_general(
+                pt_ref[i], product, (((0,), (0,)), ((), ())), preferred_element_type=jnp.float32
+            )
             out_ref[bucket, k] = galerkin.astype(jnp.bfloat16)
 
 
-def galerkin_buckets(a_blocks, ks, table, cols, prolong_t, bucket, bucket_count):
+def galerkin_buckets(a_blocks, ks, table, cols, prolong, bucket, bucket_count):
     slab_rows, unused_k, block_size, unused_size = a_blocks.shape
     n_k = len(ks)
     squeezed = pl.Squeezed()
@@ -67,7 +69,52 @@
         ),
         compiler_params=pltpu.CompilerParams(dimension_semantics=("arbitrary",)),
         cost_estimate=pl.CostEstimate(flops=flops, bytes_accessed=moved, transcendentals=0),
-    )(bucket, cols, *([a_blocks] * n_k), *([table] * (ROWS_PER_STEP * n_k)), prolong_t)
+    )(bucket, cols, *([a_blocks] * n_k), *([table] * (ROWS_PER_STEP * n_k)), prolong)
+
+
+def reduce_kernel(has_init, slot_ref, *refs):
+    if has_init:
+        init_ref, blocks_ref, out_ref = refs
+        out_ref[...] = init_ref[...]
+    else:
+        blocks_ref, out_ref = refs
+        out_ref[...] = jnp.zeros_like(out_ref)
+    slot_count = out_ref.shape[0]
+
+    def add_block(index, carry):
+        slot = slot_ref[index]
+
+        @pl.when((slot >= 0) & (slot < slot_count))
+        def _():
+            target = jnp.clip(slot, 0, slot_count - 1)
+            out_ref[target] = out_ref[target] + blocks_ref[index].astype(jnp.float32)
+
+        return carry
+
+    lax.fori_loop(0, blocks_ref.shape[0], add_block, 0)
+
+
+def reduce_by_slot(slot_of_block, blocks, init=None):
+    block_count, block_size, unused_size = blocks.shape
+    whole = lambda shape: pl.BlockSpec(shape, lambda i, s: (0,) * len(shape))
+    out_shape = (CB_DEV, block_size, block_size)
+    in_specs = [whole(blocks.shape)]
+    operands = [blocks]
+    if init is not None:
+        in_specs = [whole(out_shape)] + in_specs
+        operands = [init] + operands
+    return pl.pallas_call(
+        functools.partial(reduce_kernel, init is not None),
+        out_shape=jax.ShapeDtypeStruct(out_shape, jnp.float32),
+        grid_spec=pltpu.PrefetchScalarGridSpec(
+            num_scalar_prefetch=1, grid=(1,), in_specs=in_specs, out_specs=whole(out_shape)
+        ),
+        cost_estimate=pl.CostEstimate(
+            flops=block_count * block_size * block_size,
+            bytes_accessed=blocks.size * 2 + 8 * CB_DEV * block_size * block_size,
+            transcendentals=0,
+        ),
+    )(slot_of_block.astype(jnp.int32), *operands)
 
 
 def per_device(a_blocks, a_cols, prolong, owners, slots):
@@ -79,17 +126,24 @@
     same_owner = (owners[:, None] == owners[None, :]) & (row_ids[None, :] < row_ids[:, None])
     owner_position = jnp.sum(same_owner.astype(jnp.int32), axis=1)
     bucket = jnp.clip(owners * CAP_OWNER + owner_position, 0, bucket_count - 1).astype(jnp.int32)
-    bucket_map = jnp.arange(bucket_count, dtype=jnp.int32)[:, None] == bucket[None, :]
-    outgoing_slots = (
-        jnp.sum(jnp.where(bucket_map[:, :, None], slots[None, :, :] + 1, 0), axis=1) - 1
+    info = jnp.concatenate([owners[:, None], slots], axis=1).astype(jnp.int32)
+    all_info = lax.all_gather(info, "wide", axis=0, tiled=False)
+    src_owner = all_info[:, :, 0]
+    src_slots = all_info[:, :, 1:]
+    src_same = (src_owner[:, :, None] == src_owner[:, None, :]) & (
+        row_ids[None, None, :] < row_ids[None, :, None]
     )
-    outgoing_slots = outgoing_slots.reshape(owner_count, CAP_OWNER, per_row)
-    arrived_slots = lax.all_to_all(outgoing_slots, "wide", split_axis=0, concat_axis=0, tiled=True)
-
-    prolong_t = jnp.swapaxes(prolong, 1, 2)
+    src_position = jnp.sum(src_same.astype(jnp.int32), axis=2)
+    src_bucket = jnp.clip(src_owner * CAP_OWNER + src_position, 0, bucket_count - 1)
+    me = lax.axis_index("wide")
+    wanted = me * CAP_OWNER + jnp.arange(CAP_OWNER, dtype=jnp.int32)
+    picked = src_bucket[:, None, :] == wanted[None, :, None]
+    arrived_slots = (
+        jnp.sum(jnp.where(picked[:, :, :, None], src_slots[:, None, :, :] + 1, 0), axis=2) - 1
+    )
 
     outgoing_diag = galerkin_buckets(
-        a_blocks, (0,), prolong, row_ids[:, None], prolong_t, bucket, bucket_count
+        a_blocks, (0,), prolong, row_ids[:, None], prolong, bucket, bucket_count
     ).reshape(owner_count, CAP_OWNER, block_size, block_size)
     arrived_diag = lax.all_to_all(outgoing_diag, "wide", split_axis=0, concat_axis=0, tiled=True)
 
@@ -97,21 +151,17 @@
     piece_rows = shard_blocks.shape[0]
     off_cols = jnp.clip(a_cols[:, 1:], 0, piece_rows - 1).astype(jnp.int32)
     outgoing_off = galerkin_buckets(
-        a_blocks, tuple(range(1, per_row)), shard_blocks, off_cols, prolong_t, bucket, bucket_count
+        a_blocks, tuple(range(1, per_row)), shard_blocks, off_cols, prolong, bucket, bucket_count
     ).reshape(owner_count, CAP_OWNER * (per_row - 1), block_size, block_size)
     arrived_off = lax.all_to_all(outgoing_off, "wide", split_axis=0, concat_axis=0, tiled=True)
 
-    slots_diag = arrived_slots[:, :, :1].reshape(-1)
-    slots_off = arrived_slots[:, :, 1:].reshape(-1)
-    slot_ids = jnp.arange(CB_DEV, dtype=jnp.int32)[:, None]
-    coarse_sum = jnp.dot(
-        (slot_ids == slots_diag[None, :]).astype(jnp.bfloat16),
-        arrived_diag.reshape(-1, block_size * block_size),
-        preferred_element_type=jnp.float32,
-    ) + jnp.dot(
-        (slot_ids == slots_off[None, :]).astype(jnp.bfloat16),
-        arrived_off.reshape(-1, block_size * block_size),
-        preferred_element_type=jnp.float32,
+    coarse_diag = reduce_by_slot(
+        arrived_slots[:, :, 0].reshape(-1), arrived_diag.reshape(-1, block_size, block_size)
+    )
+    coarse_sum = reduce_by_slot(
+        arrived_slots[:, :, 1:].reshape(-1),
+        arrived_off.reshape(-1, block_size, block_size),
+        coarse_diag,
     )
     return coarse_sum.reshape(CB_DEV, block_size, block_size)
 

time: 206 us -> 248 us (1.20)
  the two profiles are of different devices: /device:TPU:7 before, /device:TPU:24 now
where the time goes in v4:
time: 248 us
  blocking collectives  136 us (55%)
  waiting for transfers between devices  43 us (17%)
  Pallas kernels  25.2 us (10%)
  starting transfers between devices  23.4 us (9%)
  between operations  13.5 us (5%)
  local copies, waits for them, and re-layouts  3.73 us (2%)
  other arithmetic  3.03 us (1%)
    all_gather x1, blocking collectives, per_device(): all_info = lax.all_gather(info, 'wide', axis=0, tiled=False)  136 us
    all_gather x1, waiting for transfers between devices, per_device(): shard_blocks = lax.all_gather(prolong, 'narrow', axis=0, tiled=True)  42.1 us
    all_to_all x1, starting transfers between devices, per_device(): lax.all_to_all(outgoing_diag, 'wide', split_axis=0, concat_axis=0, tiled=...  13.3 us
    pallas_call x2, Pallas kernels, galerkin_buckets(): pl.pallas_call(functools.partial(galerkin_kernel, n_k), out_shape=jax.Sha...  12.8 us
    pallas_call x2, Pallas kernels, reduce_by_slot(): pl.pallas_call(functools.partial(reduce_kernel, init is not None), out_sh...  12.4 us
    all_to_all x1, starting transfers between devices, per_device(): lax.all_to_all(outgoing_off, 'wide', split_axis=0, concat_axis=0, tiled=T...  10.1 us
  transfers between devices with their start and end apart: 3, of which 2 were waited for; matrix products, arithmetic and copies ran while one was open for 2% of the time, Pallas kernels for 7%

profile of v4, /device:TPU:24, one launch (start us, length us, event | category | flops | bytes accessed | tf_op | source)
XLA Modules:
  0.0 247.9 jit_solution(2307756520539367741)
XLA Ops:
  6.5 0.7 all-gather.4.cloned.1.call-update
  7.3 0.9 convert_reduce_fusion.1
  8.2 1.3 add_clamp_fusion.1.bucket_ref
  9.4 0.6 iota.30.cols_ref
  10.0 5.7 %shard_map.55 = bf16[64,1,128,128]{3,2,1,0:T(8,128)(2,1)} custom-call(s32[16]{0:T(128)} %add_clamp_fusion.1.bucket_ref, s32[16,1]{1,0:T(8,128)} %iota.30.cols_ref, bf16[16,3,128,128]{3,2,1,0:T(8,128)(2,1)} %refs_1_.3, bf16[16,128,128]{2,1,0:T(8,128)(2,1)} %refs_10_.1, bf16[16,128,128]{2,1,0:T(8,128)(2,1)} %refs_10_.1, bf16[16,128,128]{2,1,0:T(8,128)(2,1)} %refs_10_.1, ...), custom_call_target="tpu_custom_call" | custom-call | flops 134217728 | bytes 3670016 | tf_op jit(solution)/shard_map/pallas_call | solution.py:61
  15.7 13.3 %all-to-all-start = ((bf16[32,2,128,128]{3,2,1,0:T(8,128)(2,1)}), bf16[32,2,128,128]{3,2,1,0:T(8,128)(2,1)S(1)}, u32[]{:S(2)}, u32[]{:S(2)}) async-start(bf16[32,2,128,128]{3,2,1,0:T(8,128)(2,1)} %bitcast.13), calls=%async_computation | async-start | bytes 4194304 | tf_op jit(solution)/shard_map/all_to_all | solution.py:148
  29.0 0.1 copy.27
  29.1 0.6 broadcast_clamp_fusion.cols_ref
  29.7 42.1 %all-gather.4.cloned.1.call-done.refs_2_.refs_3_.refs_4_.refs_5_.refs_6_.refs_7_.refs_8_.refs_9_ = bf16[256,128,128]{2,1,0:T(8,128)(2,1)} async-done(((bf16[16,128,128]{2,1,0:T(8,128)(2,1)}), bf16[256,128,128]{2,1,0:T(8,128)(2,1)}) %all-gather.4.cloned.1.call-update) | async-done | bytes 8388624 | tf_op jit(solution)/shard_map/all_gather | solution.py:150
  71.8 7.1 %shard_map.57 = bf16[64,2,128,128]{3,2,1,0:T(8,128)(2,1)} custom-call(s32[16]{0:T(128)} %add_clamp_fusion.1.bucket_ref, s32[16,2]{1,0:T(8,128)} %broadcast_clamp_fusion.cols_ref, bf16[16,3,128,128]{3,2,1,0:T(8,128)(2,1)} %refs_1_.3, bf16[16,3,128,128]{3,2,1,0:T(8,128)(2,1)} %refs_1_.3, ...), custom_call_target="tpu_custom_call" | custom-call | flops 268435456 | bytes 6815744 | tf_op jit(solution)/shard_map/pallas_call | solution.py:61
  79.0 0.2 all-to-all-done
  79.2 1.3 copy-done
  80.5 10.1 %all-to-all-start.1 = ((bf16[32,4,128,128]{3,2,1,0:T(8,128)(2,1)}), bf16[32,4,128,128]{3,2,1,0:T(8,128)(2,1)}, u32[]{:S(2)}, u32[]{:S(2)}) async-start(bf16[32,4,128,128]{3,2,1,0:T(8,128)(2,1)} %bitcast.11), calls=%async_computation.1 | async-start | bytes 8388608 | tf_op jit(solution)/shard_map/all_to_all | solution.py:156
  90.6 136.0 %all-gather.1 = s32[32,16,4]{1,2,0:T(4,128)S(1)} all-gather(s32[1,16,4]{1,2,0:T(4,128)S(1)} %add_bitcast_fusion), channel_id=2, replica_groups=mesh['wide'=32,'narrow'=16] {'wide'}, dimensions={0}, use_global_device_ids=true | all-gather | bytes 8448 | tf_op jit(solution)/shard_map/all_gather | solution.py:130
  226.7 0.1 copy.25
  226.7 0.1 copy.26
  226.8 0.1 convert_reduce_fusion
  227.0 0.1 broadcast_compare_fusion
  227.1 0.1 copy.23
  227.2 0.6 reshape_squeeze.3.slot_ref
  227.8 0.1 copy.22
  227.9 0.7 reshape.49.slot_ref
  228.6 4.9 %shard_map.56.refs_0_ = f32[24,128,128]{2,1,0:T(8,128)} custom-call(s32[64]{0:T(128)} %reshape_squeeze.3.slot_ref, bf16[64,128,128]{2,1,0:T(8,128)(2,1)} %bitcast.12), custom_call_target="tpu_custom_call" | custom-call | flops 1048576 | bytes 5242880 | tf_op jit(solution)/shard_map/pallas_call | solution.py:106
  233.6 7.5 %shard_map.58 = f32[24,128,128]{2,1,0:T(8,128)} custom-call(s32[128]{0:T(128)} %reshape.49.slot_ref, f32[24,128,128]{2,1,0:T(8,128)} %shard_map.56.refs_0_, bf16[128,128,128]{2,1,0:T(8,128)(2,1)} %bitcast.6.refs_1_), custom_call_target="tpu_custom_call" | custom-call | flops 2097152 | bytes 7340032 | tf_op jit(solution)/shard_map/pallas_call | solution.py:106
  (21 shorter events, 0.1 us)
Async XLA Ops:
  6.5 65.3 %all-gather.4.cloned.1.call-start = ((), (), s32[]{:S(2)}) async-start(), calls=%async_computation.2 | async-start | bytes 8912896 | tf_op jit(solution)/shard_map/all_gather | solution.py:150
  15.7 13.3 %copy-start.3 = (s32[16,3]{0,1:T(4,128)S(1)}, s32[16,3]{0,1:T(4,128)}, u32[]{:S(2)}) copy-start(s32[16,3]{0,1:T(4,128)} %param.6) | copy-start | bytes 580
  15.7 63.5 %all-to-all-start = ((bf16[32,2,128,128]{3,2,1,0:T(8,128)(2,1)}), bf16[32,2,128,128]{3,2,1,0:T(8,128)(2,1)S(1)}, u32[]{:S(2)}, u32[]{:S(2)}) async-start(bf16[32,2,128,128]{3,2,1,0:T(8,128)(2,1)} %bitcast.13), calls=%async_computation | async-start | bytes 4194304 | tf_op jit(solution)/shard_map/all_to_all | solution.py:148
  79.2 1.3 copy-start
  79.2 11.4 %copy-start.1 = (s32[16,3]{0,1:T(4,128)S(1)}, s32[16,3]{0,1:T(4,128)}, u32[]{:S(2)}) copy-start(s32[16,3]{0,1:T(4,128)} %param.9) | copy-start | bytes 580
  79.2 11.5 %copy-start.2 = (s32[16]{0:T(128)S(1)}, s32[16]{0:T(128)}, u32[]{:S(2)}) copy-start(s32[16]{0:T(128)} %param.8) | copy-start | bytes 196
  80.5 153.1 %all-to-all-start.1 = ((bf16[32,4,128,128]{3,2,1,0:T(8,128)(2,1)}), bf16[32,4,128,128]{3,2,1,0:T(8,128)(2,1)}, u32[]{:S(2)}, u32[]{:S(2)}) async-start(bf16[32,4,128,128]{3,2,1,0:T(8,128)(2,1)} %bitcast.11), calls=%async_computation.1 | async-start | bytes 8388608 | tf_op jit(solution)/shard_map/all_to_all | solution.py:156
Sparse Core Ops, SparseCore 0:
  9.4 62.3 all-gather.3

commit v5 on v4

--- a/solution.py
+++ b/solution.py
@@ -150,8 +150,9 @@
     shard_blocks = lax.all_gather(prolong, "narrow", axis=0, tiled=True)
     piece_rows = shard_blocks.shape[0]
     off_cols = jnp.clip(a_cols[:, 1:], 0, piece_rows - 1).astype(jnp.int32)
+    bucket_after_info = jnp.maximum(bucket, jnp.minimum(all_info[0, 0, 0], 0))
     outgoing_off = galerkin_buckets(
-        a_blocks, tuple(range(1, per_row)), shard_blocks, off_cols, prolong, bucket, bucket_count
+        a_blocks, tuple(range(1, per_row)), shard_blocks, off_cols, prolong, bucket_after_info, bucket_count
     ).reshape(owner_count, CAP_OWNER * (per_row - 1), block_size, block_size)
     arrived_off = lax.all_to_all(outgoing_off, "wide", split_axis=0, concat_axis=0, tiled=True)
 

time: 248 us -> 228 us (0.919)
  blocking collectives: 136 us -> 55.1 us
  waiting for transfers between devices: 43 us -> 115 us
  starting transfers between devices: 23.4 us -> 11.3 us
    all_gather x1, blocking collectives: 136 us -> 55.1 us  [per_device(): all_info = lax.all_gather(info, 'wide', axis=0, tiled=False)]
    all_to_all x1, waiting for transfers between devices: 0.01 us -> 80.8 us  [per_device(): lax.all_to_all(outgoing_off, 'wide', split_axis=0, concat_axis=0, tiled=T...]
    all_gather x1, waiting for transfers between devices: 42.1 us -> 0.01 us  [per_device(): shard_blocks = lax.all_gather(prolong, 'narrow', axis=0, tiled=True)]
    all_to_all x1, waiting for transfers between devices: 0.2 us -> 33.6 us  [per_device(): lax.all_to_all(outgoing_diag, 'wide', split_axis=0, concat_axis=0, tiled=...]
    all_to_all x1, starting transfers between devices: 13.3 us -> 5.37 us  [per_device(): lax.all_to_all(outgoing_diag, 'wide', split_axis=0, concat_axis=0, tiled=...]
    all_to_all x1, starting transfers between devices: 10.1 us -> 5.91 us  [per_device(): lax.all_to_all(outgoing_off, 'wide', split_axis=0, concat_axis=0, tiled=T...]
  transfers between devices with their start and end apart: 3 -> 3, of which waited for: 2 -> 2; matrix products, arithmetic and copies ran while one was open for 2% -> 3% of each run, Pallas kernels for 7% -> 8%
where the time goes in v5:
time: 228 us
  waiting for transfers between devices  115 us (50%)
  blocking collectives  55.1 us (24%)
  Pallas kernels  24.1 us (11%)
  between operations  14.2 us (6%)
  starting transfers between devices  11.3 us (5%)
  local copies, waits for them, and re-layouts  4.15 us (2%)
  other arithmetic  3.65 us (2%)
    all_to_all x1, waiting for transfers between devices, per_device(): lax.all_to_all(outgoing_off, 'wide', split_axis=0, concat_axis=0, tiled=T...  80.8 us
    all_gather x1, blocking collectives, per_device(): all_info = lax.all_gather(info, 'wide', axis=0, tiled=False)  55.1 us
    all_to_all x1, waiting for transfers between devices, per_device(): lax.all_to_all(outgoing_diag, 'wide', split_axis=0, concat_axis=0, tiled=...  33.6 us
    pallas_call x2, Pallas kernels, galerkin_buckets(): pl.pallas_call(functools.partial(galerkin_kernel, n_k), out_shape=jax.Sha...  12.8 us
    pallas_call x2, Pallas kernels, reduce_by_slot(): pl.pallas_call(functools.partial(reduce_kernel, init is not None), out_sh...  11.2 us
    all_to_all x1, starting transfers between devices, per_device(): lax.all_to_all(outgoing_off, 'wide', split_axis=0, concat_axis=0, tiled=T...  5.91 us
    all_to_all x1, starting transfers between devices, per_device(): lax.all_to_all(outgoing_diag, 'wide', split_axis=0, concat_axis=0, tiled=...  5.37 us
  transfers between devices with their start and end apart: 3, of which 2 were waited for; matrix products, arithmetic and copies ran while one was open for 3% of the time, Pallas kernels for 8%

profile of v5, /device:TPU:24, one launch (start us, length us, event | category | flops | bytes accessed | tf_op | source)
XLA Modules:
  0.0 227.5 jit_solution(1188162781554223805)
XLA Ops:
  6.5 0.7 all-gather.4.cloned.1.call-update
  7.3 0.7 add_bitcast_fusion
  7.9 55.1 %all-gather.1 = s32[32,16,4]{1,2,0:T(4,128)S(1)} all-gather(s32[1,16,4]{1,2,0:T(4,128)S(1)} %add_bitcast_fusion), channel_id=2, replica_groups=mesh['wide'=32,'narrow'=16] {'wide'}, dimensions={0}, use_global_device_ids=true | all-gather | bytes 8448 | tf_op jit(solution)/shard_map/all_gather | solution.py:130
  63.0 0.5 slice.28
  64.2 0.9 convert_reduce_fusion.1
  65.1 1.2 broadcast_maximum_fusion
  66.3 0.6 iota.30.cols_ref
  66.9 5.7 %shard_map.55 = bf16[64,1,128,128]{3,2,1,0:T(8,128)(2,1)} custom-call(s32[16]{0:T(128)} %get-tuple-element.6.bucket_ref, s32[16,1]{1,0:T(8,128)} %iota.30.cols_ref, bf16[16,3,128,128]{3,2,1,0:T(8,128)(2,1)} %refs_1_.3, bf16[16,128,128]{2,1,0:T(8,128)(2,1)} %refs_10_.1, bf16[16,128,128]{2,1,0:T(8,128)(2,1)} %refs_10_.1, bf16[16,128,128]{2,1,0:T(8,128)(2,1)} %refs_10_.1, ...), custom_call_target="tpu_custom_call" | custom-call | flops 134217728 | bytes 3670016 | tf_op jit(solution)/shard_map/pallas_call | solution.py:61
  72.5 5.4 %all-to-all-start = ((bf16[32,2,128,128]{3,2,1,0:T(8,128)(2,1)}), bf16[32,2,128,128]{3,2,1,0:T(8,128)(2,1)S(1)}, u32[]{:S(2)}, u32[]{:S(2)}) async-start(bf16[32,2,128,128]{3,2,1,0:T(8,128)(2,1)} %bitcast.14), calls=%async_computation | async-start | bytes 4194304 | tf_op jit(solution)/shard_map/all_to_all | solution.py:148
  78.0 0.1 copy.27
  78.0 0.6 broadcast_clamp_fusion.cols_ref
  78.6 7.1 %shard_map.57 = bf16[64,2,128,128]{3,2,1,0:T(8,128)(2,1)} custom-call(s32[16]{0:T(128)} %get-tuple-element.5.bucket_ref, s32[16,2]{1,0:T(8,128)} %broadcast_clamp_fusion.cols_ref, bf16[16,3,128,128]{3,2,1,0:T(8,128)(2,1)} %refs_1_.3, bf16[16,3,128,128]{3,2,1,0:T(8,128)(2,1)} %refs_1_.3, ...), custom_call_target="tpu_custom_call" | custom-call | flops 268435456 | bytes 6815744 | tf_op jit(solution)/shard_map/pallas_call | solution.py:61
  85.8 33.6 %all-to-all-done = bf16[32,2,128,128]{3,2,1,0:T(8,128)(2,1)S(1)} async-done(((bf16[32,2,128,128]{3,2,1,0:T(8,128)(2,1)}), bf16[32,2,128,128]{3,2,1,0:T(8,128)(2,1)S(1)}, u32[]{:S(2)}, u32[]{:S(2)}) %all-to-all-start) | async-done | bytes 2097184 | tf_op jit(solution)/shard_map/all_to_all | solution.py:148
  119.4 1.3 copy-done
  120.7 5.9 %all-to-all-start.1 = ((bf16[32,4,128,128]{3,2,1,0:T(8,128)(2,1)}), bf16[32,4,128,128]{3,2,1,0:T(8,128)(2,1)}, u32[]{:S(2)}, u32[]{:S(2)}) async-start(bf16[32,4,128,128]{3,2,1,0:T(8,128)(2,1)} %bitcast.12), calls=%async_computation.1 | async-start | bytes 8388608 | tf_op jit(solution)/shard_map/all_to_all | solution.py:157
  126.8 0.1 copy.26
  126.9 0.1 convert_reduce_fusion
  127.1 0.1 copy.23
  127.2 0.6 reshape_squeeze.3.slot_ref
  127.8 0.1 copy.22
  128.0 0.6 reshape.51.slot_ref
  128.6 4.6 %shard_map.56.refs_0_ = f32[24,128,128]{2,1,0:T(8,128)} custom-call(s32[64]{0:T(128)} %reshape_squeeze.3.slot_ref, bf16[64,128,128]{2,1,0:T(8,128)(2,1)} %bitcast.13), custom_call_target="tpu_custom_call" | custom-call | flops 1048576 | bytes 5242880 | tf_op jit(solution)/shard_map/pallas_call | solution.py:106
  133.1 80.8 %all-to-all-done.1 = bf16[32,4,128,128]{3,2,1,0:T(8,128)(2,1)} async-done(((bf16[32,4,128,128]{3,2,1,0:T(8,128)(2,1)}), bf16[32,4,128,128]{3,2,1,0:T(8,128)(2,1)}, u32[]{:S(2)}, u32[]{:S(2)}) %all-to-all-start.1) | async-done | bytes 4194336 | tf_op jit(solution)/shard_map/all_to_all | solution.py:157
  214.0 6.7 %shard_map.58 = f32[24,128,128]{2,1,0:T(8,128)} custom-call(s32[128]{0:T(128)} %reshape.51.slot_ref, f32[24,128,128]{2,1,0:T(8,128)} %shard_map.56.refs_0_, bf16[128,128,128]{2,1,0:T(8,128)(2,1)} %bitcast.7.refs_1_), custom_call_target="tpu_custom_call" | custom-call | flops 2097152 | bytes 7340032 | tf_op jit(solution)/shard_map/pallas_call | solution.py:106
  (18 shorter events, 0.3 us)
Async XLA Ops:
  6.5 72.1 %all-gather.4.cloned.1.call-start = ((), (), s32[]{:S(2)}) async-start(), calls=%async_computation.2 | async-start | bytes 8912896 | tf_op jit(solution)/shard_map/all_gather | solution.py:150
  72.5 5.4 %copy-start.1 = (s32[16,3]{0,1:T(4,128)S(1)}, s32[16,3]{0,1:T(4,128)}, u32[]{:S(2)}) copy-start(s32[16,3]{0,1:T(4,128)} %param.6) | copy-start | bytes 580
  72.5 46.9 %all-to-all-start = ((bf16[32,2,128,128]{3,2,1,0:T(8,128)(2,1)}), bf16[32,2,128,128]{3,2,1,0:T(8,128)(2,1)S(1)}, u32[]{:S(2)}, u32[]{:S(2)}) async-start(bf16[32,2,128,128]{3,2,1,0:T(8,128)(2,1)} %bitcast.14), calls=%async_computation | async-start | bytes 4194304 | tf_op jit(solution)/shard_map/all_to_all | solution.py:148
  119.4 1.3 copy-start
  120.7 93.3 %all-to-all-start.1 = ((bf16[32,4,128,128]{3,2,1,0:T(8,128)(2,1)}), bf16[32,4,128,128]{3,2,1,0:T(8,128)(2,1)}, u32[]{:S(2)}, u32[]{:S(2)}) async-start(bf16[32,4,128,128]{3,2,1,0:T(8,128)(2,1)} %bitcast.12), calls=%async_computation.1 | async-start | bytes 8388608 | tf_op jit(solution)/shard_map/all_to_all | solution.py:157
Sparse Core Ops, SparseCore 0:
  9.4 62.3 all-gather.3

commit v6 on v4

--- a/solution.py
+++ b/solution.py
@@ -126,21 +126,12 @@
     same_owner = (owners[:, None] == owners[None, :]) & (row_ids[None, :] < row_ids[:, None])
     owner_position = jnp.sum(same_owner.astype(jnp.int32), axis=1)
     bucket = jnp.clip(owners * CAP_OWNER + owner_position, 0, bucket_count - 1).astype(jnp.int32)
-    info = jnp.concatenate([owners[:, None], slots], axis=1).astype(jnp.int32)
-    all_info = lax.all_gather(info, "wide", axis=0, tiled=False)
-    src_owner = all_info[:, :, 0]
-    src_slots = all_info[:, :, 1:]
-    src_same = (src_owner[:, :, None] == src_owner[:, None, :]) & (
-        row_ids[None, None, :] < row_ids[None, :, None]
+    bucket_map = jnp.arange(bucket_count, dtype=jnp.int32)[:, None] == bucket[None, :]
+    outgoing_slots = (
+        jnp.sum(jnp.where(bucket_map[:, :, None], slots[None, :, :] + 1, 0), axis=1) - 1
     )
-    src_position = jnp.sum(src_same.astype(jnp.int32), axis=2)
-    src_bucket = jnp.clip(src_owner * CAP_OWNER + src_position, 0, bucket_count - 1)
-    me = lax.axis_index("wide")
-    wanted = me * CAP_OWNER + jnp.arange(CAP_OWNER, dtype=jnp.int32)
-    picked = src_bucket[:, None, :] == wanted[None, :, None]
-    arrived_slots = (
-        jnp.sum(jnp.where(picked[:, :, :, None], src_slots[:, None, :, :] + 1, 0), axis=2) - 1
-    )
+    outgoing_slots = outgoing_slots.reshape(owner_count, CAP_OWNER, per_row)
+    arrived_slots = lax.all_to_all(outgoing_slots, "wide", split_axis=0, concat_axis=0, tiled=True)
 
     outgoing_diag = galerkin_buckets(
         a_blocks, (0,), prolong, row_ids[:, None], prolong, bucket, bucket_count

time: 248 us -> 205 us (0.83)
  the two profiles are of different devices: /device:TPU:24 before, /device:TPU:7 now
where the time goes in v6:
time: 205 us; the launch traced here: 203 us
  waiting for transfers between devices  132 us (64%)
  starting transfers between devices  25.9 us (13%)
  Pallas kernels  24.1 us (12%)
  between operations  13.5 us (7%)
  local copies, waits for them, and re-layouts  4.77 us (2%)
  other arithmetic  3.04 us (1%)
    all_to_all x1, waiting for transfers between devices, per_device(): lax.all_to_all(outgoing_off, 'wide', split_axis=0, concat_axis=0, tiled=T...  88.1 us
    all_gather x1, waiting for transfers between devices, per_device(): shard_blocks = lax.all_gather(prolong, 'narrow', axis=0, tiled=True)  33.2 us
    all_to_all x1, starting transfers between devices, per_device(): lax.all_to_all(outgoing_slots, 'wide', split_axis=0, concat_axis=0, tiled...  12.8 us
    pallas_call x2, Pallas kernels, galerkin_buckets(): pl.pallas_call(functools.partial(galerkin_kernel, n_k), out_shape=jax.Sha...  12.8 us
    pallas_call x2, Pallas kernels, reduce_by_slot(): pl.pallas_call(functools.partial(reduce_kernel, init is not None), out_sh...  11.3 us
    all_to_all x1, waiting for transfers between devices, per_device(): lax.all_to_all(outgoing_diag, 'wide', split_axis=0, concat_axis=0, tiled=...  8.87 us
    all_to_all x1, starting transfers between devices, per_device(): lax.all_to_all(outgoing_diag, 'wide', split_axis=0, concat_axis=0, tiled=...  8.21 us
    all_to_all x1, starting transfers between devices, per_device(): lax.all_to_all(outgoing_off, 'wide', split_axis=0, concat_axis=0, tiled=T...  4.85 us
  transfers between devices with their start and end apart: 4, of which 4 were waited for; matrix products, arithmetic and copies ran while one was open for 3% of the time, Pallas kernels for 9%

profile of v6, /device:TPU:7, one launch (start us, length us, event | category | flops | bytes accessed | tf_op | source)
XLA Modules:
  0.0 203.2 jit_solution(9541160205602699487)
XLA Ops:
  6.5 0.7 all-gather.2.cloned.1.call-update
  7.3 0.9 convert_reduce_fusion
  8.2 0.7 add_clamp_fusion.bucket_ref
  8.9 0.7 broadcast_add_fusion.1
  9.6 0.1 select_reduce_fusion
  9.7 0.7 copy.17
  10.4 12.8 %all-to-all-start = ((s32[32,2,3]{2,1,0:T(2,128)}), s32[32,2,3]{2,1,0:T(2,128)S(1)}, u32[]{:S(2)}, u32[]{:S(2)}) async-start(s32[32,2,3]{2,1,0:T(2,128)} %bitcast), calls=%async_computation | async-start | bytes 65536 | tf_op jit(solution)/shard_map/all_to_all | solution.py:134
  23.3 0.6 iota.17.cols_ref
  23.9 5.7 %shard_map.55 = bf16[64,1,128,128]{3,2,1,0:T(8,128)(2,1)} custom-call(s32[16]{0:T(128)} %copy-done.1, s32[16,1]{1,0:T(8,128)} %iota.17.cols_ref, bf16[16,3,128,128]{3,2,1,0:T(8,128)(2,1)} %refs_1_.3, bf16[16,128,128]{2,1,0:T(8,128)(2,1)} %refs_10_.1, bf16[16,128,128]{2,1,0:T(8,128)(2,1)} %refs_10_.1, bf16[16,128,128]{2,1,0:T(8,128)(2,1)} %refs_10_.1, ...), custom_call_target="tpu_custom_call" | custom-call | flops 134217728 | bytes 3670016 | tf_op jit(solution)/shard_map/pallas_call | solution.py:61
  29.5 1.0 all-to-all-done
  30.6 8.2 %all-to-all-start.1 = ((bf16[32,2,128,128]{3,2,1,0:T(8,128)(2,1)}), bf16[32,2,128,128]{3,2,1,0:T(8,128)(2,1)S(1)}, u32[]{:S(2)}, u32[]{:S(2)}) async-start(bf16[32,2,128,128]{3,2,1,0:T(8,128)(2,1)} %bitcast.7), calls=%async_computation.1 | async-start | bytes 4194304 | tf_op jit(solution)/shard_map/all_to_all | solution.py:139
  38.9 0.6 broadcast_clamp_fusion.cols_ref
  39.5 33.2 %all-gather.2.cloned.1.call-done.refs_2_.refs_3_.refs_4_.refs_5_.refs_6_.refs_7_.refs_8_.refs_9_ = bf16[256,128,128]{2,1,0:T(8,128)(2,1)} async-done(((bf16[16,128,128]{2,1,0:T(8,128)(2,1)}), bf16[256,128,128]{2,1,0:T(8,128)(2,1)}) %all-gather.2.cloned.1.call-update) | async-done | bytes 8388624 | tf_op jit(solution)/shard_map/all_gather | solution.py:141
  72.6 7.1 %shard_map.57 = bf16[64,2,128,128]{3,2,1,0:T(8,128)(2,1)} custom-call(s32[16]{0:T(128)} %copy-done.1, s32[16,2]{1,0:T(8,128)} %broadcast_clamp_fusion.cols_ref, bf16[16,3,128,128]{3,2,1,0:T(8,128)(2,1)} %refs_1_.3, bf16[16,3,128,128]{3,2,1,0:T(8,128)(2,1)} %refs_1_.3, ...), custom_call_target="tpu_custom_call" | custom-call | flops 268435456 | bytes 6815744 | tf_op jit(solution)/shard_map/pallas_call | solution.py:61
  79.8 8.9 %all-to-all-done.1 = bf16[32,2,128,128]{3,2,1,0:T(8,128)(2,1)S(1)} async-done(((bf16[32,2,128,128]{3,2,1,0:T(8,128)(2,1)}), bf16[32,2,128,128]{3,2,1,0:T(8,128)(2,1)S(1)}, u32[]{:S(2)}, u32[]{:S(2)}) %all-to-all-start.1) | async-done | bytes 2097184 | tf_op jit(solution)/shard_map/all_to_all | solution.py:139
  88.7 1.3 copy-done
  90.0 4.9 %all-to-all-start.2 = ((bf16[32,4,128,128]{3,2,1,0:T(8,128)(2,1)}), bf16[32,4,128,128]{3,2,1,0:T(8,128)(2,1)}, u32[]{:S(2)}, u32[]{:S(2)}) async-start(bf16[32,4,128,128]{3,2,1,0:T(8,128)(2,1)} %bitcast.5), calls=%async_computation.2 | async-start | bytes 8388608 | tf_op jit(solution)/shard_map/all_to_all | solution.py:147
  94.8 0.6 slice_reduce_fusion
  95.4 0.6 reshape_squeeze.3.slot_ref
  96.1 0.1 slice.12
  96.2 0.7 reshape.41.slot_ref
  96.9 4.6 %shard_map.56.refs_0_ = f32[24,128,128]{2,1,0:T(8,128)} custom-call(s32[64]{0:T(128)} %reshape_squeeze.3.slot_ref, bf16[64,128,128]{2,1,0:T(8,128)(2,1)} %bitcast.6), custom_call_target="tpu_custom_call" | custom-call | flops 1048576 | bytes 5242880 | tf_op jit(solution)/shard_map/pallas_call | solution.py:106
  101.5 88.1 %all-to-all-done.2 = bf16[32,4,128,128]{3,2,1,0:T(8,128)(2,1)} async-done(((bf16[32,4,128,128]{3,2,1,0:T(8,128)(2,1)}), bf16[32,4,128,128]{3,2,1,0:T(8,128)(2,1)}, u32[]{:S(2)}, u32[]{:S(2)}) %all-to-all-start.2) | async-done | bytes 4194336 | tf_op jit(solution)/shard_map/all_to_all | solution.py:147
  189.6 6.7 %shard_map.58 = f32[24,128,128]{2,1,0:T(8,128)} custom-call(s32[128]{0:T(128)} %reshape.41.slot_ref, f32[24,128,128]{2,1,0:T(8,128)} %shard_map.56.refs_0_, bf16[128,128,128]{2,1,0:T(8,128)(2,1)} %bitcast.4.refs_1_), custom_call_target="tpu_custom_call" | custom-call | flops 2097152 | bytes 7340032 | tf_op jit(solution)/shard_map/pallas_call | solution.py:106
  (10 shorter events, 0.2 us)
Async XLA Ops:
  6.5 66.1 %all-gather.2.cloned.1.call-start = ((), (), s32[]{:S(2)}) async-start(), calls=%async_computation.3 | async-start | bytes 8912896 | tf_op jit(solution)/shard_map/all_gather | solution.py:141
  8.8 15.0 %copy-start.1 = (s32[16]{0:T(128)}, s32[16]{0:T(128)S(1)}, u32[]{:S(2)}) copy-start(s32[16]{0:T(128)S(1)} %add_clamp_fusion.bucket_ref) | copy-start | bytes 196
  10.4 20.1 %all-to-all-start = ((s32[32,2,3]{2,1,0:T(2,128)}), s32[32,2,3]{2,1,0:T(2,128)S(1)}, u32[]{:S(2)}, u32[]{:S(2)}) async-start(s32[32,2,3]{2,1,0:T(2,128)} %bitcast), calls=%async_computation | async-start | bytes 65536 | tf_op jit(solution)/shard_map/all_to_all | solution.py:134
  30.6 8.2 %copy-start.2 = (s32[16,3]{0,1:T(4,128)S(1)}, s32[16,3]{0,1:T(4,128)}, u32[]{:S(2)}) copy-start(s32[16,3]{0,1:T(4,128)} %param.6) | copy-start | bytes 580
  30.6 58.1 %all-to-all-start.1 = ((bf16[32,2,128,128]{3,2,1,0:T(8,128)(2,1)}), bf16[32,2,128,128]{3,2,1,0:T(8,128)(2,1)S(1)}, u32[]{:S(2)}, u32[]{:S(2)}) async-start(bf16[32,2,128,128]{3,2,1,0:T(8,128)(2,1)} %bitcast.7), calls=%async_computation.1 | async-start | bytes 4194304 | tf_op jit(solution)/shard_map/all_to_all | solution.py:139
  88.7 1.3 copy-start
  90.0 99.6 %all-to-all-start.2 = ((bf16[32,4,128,128]{3,2,1,0:T(8,128)(2,1)}), bf16[32,4,128,128]{3,2,1,0:T(8,128)(2,1)}, u32[]{:S(2)}, u32[]{:S(2)}) async-start(bf16[32,4,128,128]{3,2,1,0:T(8,128)(2,1)} %bitcast.5), calls=%async_computation.2 | async-start | bytes 8388608 | tf_op jit(solution)/shard_map/all_to_all | solution.py:147
Sparse Core Ops, SparseCore 0:
  9.4 63.1 all-gather.1

commit v7 on v6

--- a/solution.py
+++ b/solution.py
@@ -35,6 +35,66 @@
                 pt_ref[i], product, (((0,), (0,)), ((), ())), preferred_element_type=jnp.float32
             )
             out_ref[bucket, k] = galerkin.astype(jnp.bfloat16)
+
+
+META_ROWS = 16
+
+
+def diag_kernel(bucket_ref, slot_ref, a_ref, p_ref, out_ref):
+    step = pl.program_id(0)
+    block_size = p_ref.shape[-1]
+    per_row = slot_ref.shape[1]
+
+    @pl.when(step == 0)
+    def _():
+        out_ref[...] = jnp.zeros_like(out_ref)
+
+    rows = lax.broadcasted_iota(jnp.int32, (META_ROWS, block_size), 0)
+    cols = lax.broadcasted_iota(jnp.int32, (META_ROWS, block_size), 1)
+    for i in range(ROWS_PER_STEP):
+        row = step * ROWS_PER_STEP + i
+        bucket = bucket_ref[row]
+        owner = bucket // CAP_OWNER
+        pos = bucket - owner * CAP_OWNER
+        product = jnp.dot(a_ref[i], p_ref[i], preferred_element_type=jnp.float32).astype(jnp.bfloat16)
+        galerkin = lax.dot_general(
+            p_ref[i], product, (((0,), (0,)), ((), ())), preferred_element_type=jnp.float32
+        )
+        out_ref[owner, pl.ds(pl.multiple_of(pos * block_size, block_size), block_size), :] = (
+            galerkin.astype(jnp.bfloat16)
+        )
+        meta = jnp.zeros((META_ROWS, block_size), jnp.int32)
+        for k in range(per_row):
+            meta = jnp.where((rows == 0) & (cols == pos * per_row + k), slot_ref[row, k] + 1, meta)
+        meta_rows = pl.ds(CAP_OWNER * block_size, META_ROWS)
+        out_ref[owner, meta_rows, :] = (
+            out_ref[owner, meta_rows, :].astype(jnp.float32) + meta.astype(jnp.float32)
+        ).astype(jnp.bfloat16)
+
+
+def diag_buckets(a_blocks, prolong, slots, bucket, owner_count):
+    slab_rows, per_row, block_size, unused_size = a_blocks.shape
+    squeezed = pl.Squeezed()
+    chunk_rows = CAP_OWNER * block_size + META_ROWS
+    return pl.pallas_call(
+        diag_kernel,
+        out_shape=jax.ShapeDtypeStruct((owner_count, chunk_rows, block_size), jnp.bfloat16),
+        grid_spec=pltpu.PrefetchScalarGridSpec(
+            num_scalar_prefetch=2,
+            grid=(slab_rows // ROWS_PER_STEP,),
+            in_specs=[
+                pl.BlockSpec((ROWS_PER_STEP, squeezed, block_size, block_size), lambda s, b, c: (s, 0, 0, 0)),
+                pl.BlockSpec((ROWS_PER_STEP, block_size, block_size), lambda s, b, c: (s, 0, 0)),
+            ],
+            out_specs=pl.BlockSpec((owner_count, chunk_rows, block_size), lambda s, b, c: (0, 0, 0)),
+        ),
+        compiler_params=pltpu.CompilerParams(dimension_semantics=("arbitrary",)),
+        cost_estimate=pl.CostEstimate(
+            flops=4 * slab_rows * block_size ** 3,
+            bytes_accessed=2 * block_size * (2 * slab_rows * block_size + owner_count * chunk_rows),
+            transcendentals=0,
+        ),
+    )(bucket, slots.astype(jnp.int32), a_blocks, prolong)
 
 
 def galerkin_buckets(a_blocks, ks, table, cols, prolong, bucket, bucket_count):
@@ -126,17 +186,12 @@
     same_owner = (owners[:, None] == owners[None, :]) & (row_ids[None, :] < row_ids[:, None])
     owner_position = jnp.sum(same_owner.astype(jnp.int32), axis=1)
     bucket = jnp.clip(owners * CAP_OWNER + owner_position, 0, bucket_count - 1).astype(jnp.int32)
-    bucket_map = jnp.arange(bucket_count, dtype=jnp.int32)[:, None] == bucket[None, :]
-    outgoing_slots = (
-        jnp.sum(jnp.where(bucket_map[:, :, None], slots[None, :, :] + 1, 0), axis=1) - 1
-    )
-    outgoing_slots = outgoing_slots.reshape(owner_count, CAP_OWNER, per_row)
-    arrived_slots = lax.all_to_all(outgoing_slots, "wide", split_axis=0, concat_axis=0, tiled=True)
-
-    outgoing_diag = galerkin_buckets(
-        a_blocks, (0,), prolong, row_ids[:, None], prolong, bucket, bucket_count
-    ).reshape(owner_count, CAP_OWNER, block_size, block_size)
+    outgoing_diag = diag_buckets(a_blocks, prolong, slots, bucket, owner_count)
     arrived_diag = lax.all_to_all(outgoing_diag, "wide", split_axis=0, concat_axis=0, tiled=True)
+    arrived_meta = arrived_diag[:, CAP_OWNER * block_size, : CAP_OWNER * per_row].astype(jnp.float32)
+    arrived_slots = (jnp.round(arrived_meta).astype(jnp.int32) - 1).reshape(
+        owner_count, CAP_OWNER, per_row
+    )
 
     shard_blocks = lax.all_gather(prolong, "narrow", axis=0, tiled=True)
     piece_rows = shard_blocks.shape[0]
@@ -147,7 +202,8 @@
     arrived_off = lax.all_to_all(outgoing_off, "wide", split_axis=0, concat_axis=0, tiled=True)
 
     coarse_diag = reduce_by_slot(
-        arrived_slots[:, :, 0].reshape(-1), arrived_diag.reshape(-1, block_size, block_size)
+        arrived_slots[:, :, 0].reshape(-1),
+        arrived_diag[:, : CAP_OWNER * block_size].reshape(-1, block_size, block_size),
     )
     coarse_sum = reduce_by_slot(
         arrived_slots[:, :, 1:].reshape(-1),

time: 205 us -> 202 us (0.985)
  the two profiles are of different devices: /device:TPU:7 before, /device:TPU:3 now
where the time goes in v7:
time: 202 us; the launch traced here: 201 us
  waiting for transfers between devices  135 us (67%)
  Pallas kernels  24 us (12%)
  starting transfers between devices  21.4 us (11%)
  between operations  13.4 us (7%)
  local copies, waits for them, and re-layouts  4.67 us (2%)
  other arithmetic  2.77 us (1%)
    all_to_all x1, waiting for transfers between devices, per_device(): lax.all_to_all(outgoing_off, 'wide', split_axis=0, concat_axis=0, tiled=T...  90 us
    all_gather x1, waiting for transfers between devices, per_device(): shard_blocks = lax.all_gather(prolong, 'narrow', axis=0, tiled=True)  42.7 us
    all_to_all x1, starting transfers between devices, per_device(): lax.all_to_all(outgoing_diag, 'wide', split_axis=0, concat_axis=0, tiled=...  13 us
    pallas_call x2, Pallas kernels, reduce_by_slot(): pl.pallas_call(functools.partial(reduce_kernel, init is not None), out_sh...  11.4 us
    all_to_all x1, starting transfers between devices, per_device(): lax.all_to_all(outgoing_off, 'wide', split_axis=0, concat_axis=0, tiled=T...  8.38 us
    pallas_call x1, Pallas kernels, galerkin_buckets(): pl.pallas_call(functools.partial(galerkin_kernel, n_k), out_shape=jax.Sha...  7.15 us
    pallas_call x1, Pallas kernels, diag_buckets(): pl.pallas_call(diag_kernel, out_shape=jax.ShapeDtypeStruct((owner_count,...  5.48 us
  transfers between devices with their start and end apart: 3, of which 3 were waited for; matrix products, arithmetic and copies ran while one was open for 4% of the time, Pallas kernels for 9%

profile of v7, /device:TPU:3, one launch (start us, length us, event | category | flops | bytes accessed | tf_op | source)
XLA Modules:
  0.0 201.4 jit_solution(12277888637215516038)
XLA Ops:
  6.5 0.0 all-gather.2.cloned.1.call-start
  6.5 0.7 all-gather.2.cloned.1.call-update
  7.3 1.4 copy.24.slot_ref
  8.6 0.9 convert_reduce_fusion
  9.5 1.2 add_clamp_fusion.bucket_ref
  10.8 5.5 %shard_map.55 = bf16[32,272,128]{2,1,0:T(8,128)(2,1)} custom-call(s32[16]{0:T(128)} %add_clamp_fusion.bucket_ref, s32[16,3]{1,0:T(8,128)} %copy.24.slot_ref, bf16[16,3,128,128]{3,2,1,0:T(8,128)(2,1)} %refs_1_.1, bf16[16,128,128]{2,1,0:T(8,128)(2,1)} %refs_10_.1), custom_call_target="tpu_custom_call" | custom-call | flops 134217728 | bytes 3276800 | tf_op jit(solution)/shard_map/pallas_call | solution.py:79
  16.2 0.0 copy-start
  16.2 13.0 %all-to-all-start = ((bf16[32,272,128]{2,1,0:T(8,128)(2,1)}), bf16[32,272,128]{2,1,0:T(8,128)(2,1)S(1)}, u32[]{:S(2)}, u32[]{:S(2)}) async-start(bf16[32,272,128]{2,1,0:T(8,128)(2,1)} %shard_map.55), calls=%async_computation | async-start | bytes 4456448 | tf_op jit(solution)/shard_map/all_to_all | solution.py:190
  29.3 0.0 copy-done
  29.3 0.1 copy.29
  29.4 0.6 broadcast_clamp_fusion.cols_ref
  30.0 42.7 %all-gather.2.cloned.1.call-done.refs_2_.refs_3_.refs_4_.refs_5_.refs_6_.refs_7_.refs_8_.refs_9_ = bf16[256,128,128]{2,1,0:T(8,128)(2,1)} async-done(((bf16[16,128,128]{2,1,0:T(8,128)(2,1)}), bf16[256,128,128]{2,1,0:T(8,128)(2,1)}) %all-gather.2.cloned.1.call-update) | async-done | bytes 8388624 | tf_op jit(solution)/shard_map/all_gather | solution.py:196
  72.7 7.1 %shard_map.57 = bf16[64,2,128,128]{3,2,1,0:T(8,128)(2,1)} custom-call(s32[16]{0:T(128)} %add_clamp_fusion.bucket_ref, s32[16,2]{1,0:T(8,128)} %broadcast_clamp_fusion.cols_ref, bf16[16,3,128,128]{3,2,1,0:T(8,128)(2,1)} %refs_1_.1, bf16[16,3,128,128]{3,2,1,0:T(8,128)(2,1)} %refs_1_.1, ...), custom_call_target="tpu_custom_call" | custom-call | flops 268435456 | bytes 6815744 | tf_op jit(solution)/shard_map/pallas_call | solution.py:121
  79.8 1.6 all-to-all-done
  81.5 8.4 %all-to-all-start.1 = ((bf16[32,4,128,128]{3,2,1,0:T(8,128)(2,1)}), bf16[32,4,128,128]{3,2,1,0:T(8,128)(2,1)}, u32[]{:S(2)}, u32[]{:S(2)}) async-start(bf16[32,4,128,128]{3,2,1,0:T(8,128)(2,1)} %bitcast.7), calls=%async_computation.1 | async-start | bytes 8388608 | tf_op jit(solution)/shard_map/all_to_all | solution.py:202
  89.9 0.1 copy.25
  90.0 0.1 copy.27
  90.1 0.6 reshape_squeeze.3.slot_ref
  90.7 0.1 copy.26
  90.8 0.7 reshape.21.slot_ref
  91.5 1.6 slice.23
  93.1 4.6 %shard_map.56.refs_0_ = f32[24,128,128]{2,1,0:T(8,128)} custom-call(s32[64]{0:T(128)} %reshape_squeeze.3.slot_ref, bf16[64,128,128]{2,1,0:T(8,128)(2,1)} %bitcast.8), custom_call_target="tpu_custom_call" | custom-call | flops 1048576 | bytes 5242880 | tf_op jit(solution)/shard_map/pallas_call | solution.py:166
  97.7 90.0 %all-to-all-done.1 = bf16[32,4,128,128]{3,2,1,0:T(8,128)(2,1)} async-done(((bf16[32,4,128,128]{3,2,1,0:T(8,128)(2,1)}), bf16[32,4,128,128]{3,2,1,0:T(8,128)(2,1)}, u32[]{:S(2)}, u32[]{:S(2)}) %all-to-all-start.1) | async-done | bytes 4194336 | tf_op jit(solution)/shard_map/all_to_all | solution.py:202
  187.8 6.8 %shard_map.58 = f32[24,128,128]{2,1,0:T(8,128)} custom-call(s32[128]{0:T(128)} %reshape.21.slot_ref, f32[24,128,128]{2,1,0:T(8,128)} %shard_map.56.refs_0_, bf16[128,128,128]{2,1,0:T(8,128)(2,1)} %bitcast.2.refs_1_), custom_call_target="tpu_custom_call" | custom-call | flops 2097152 | bytes 7340032 | tf_op jit(solution)/shard_map/pallas_call | solution.py:166
  (5 shorter events, 0.0 us)
Async XLA Ops:
  6.5 66.1 %all-gather.2.cloned.1.call-start = ((), (), s32[]{:S(2)}) async-start(), calls=%async_computation.2 | async-start | bytes 8912896 | tf_op jit(solution)/shard_map/all_gather | solution.py:196
  16.2 13.0 %copy-start = (s32[16,3]{0,1:T(4,128)S(1)}, s32[16,3]{0,1:T(4,128)}, u32[]{:S(2)}) copy-start(s32[16,3]{0,1:T(4,128)} %param.6) | copy-start | bytes 580
  16.2 65.2 %all-to-all-start = ((bf16[32,272,128]{2,1,0:T(8,128)(2,1)}), bf16[32,272,128]{2,1,0:T(8,128)(2,1)S(1)}, u32[]{:S(2)}, u32[]{:S(2)}) async-start(bf16[32,272,128]{2,1,0:T(8,128)(2,1)} %shard_map.55), calls=%async_computation | async-start | bytes 4456448 | tf_op jit(solution)/shard_map/all_to_all | solution.py:190
  81.5 106.3 %all-to-all-start.1 = ((bf16[32,4,128,128]{3,2,1,0:T(8,128)(2,1)}), bf16[32,4,128,128]{3,2,1,0:T(8,128)(2,1)}, u32[]{:S(2)}, u32[]{:S(2)}) async-start(bf16[32,4,128,128]{3,2,1,0:T(8,128)(2,1)} %bitcast.7), calls=%async_computation.1 | async-start | bytes 8388608 | tf_op jit(solution)/shard_map/all_to_all | solution.py:202
Sparse Core Ops, SparseCore 0:
  9.4 63.1 all-gather.1

commit v8 on v7

--- a/solution.py
+++ b/solution.py
@@ -40,10 +40,9 @@
 META_ROWS = 16
 
 
-def diag_kernel(bucket_ref, slot_ref, a_ref, p_ref, out_ref):
+def diag_kernel(per_row, bucket_ref, slot_ref, a_ref, p_ref, out_ref):
     step = pl.program_id(0)
     block_size = p_ref.shape[-1]
-    per_row = slot_ref.shape[1]
 
     @pl.when(step == 0)
     def _():
@@ -77,7 +76,7 @@
     squeezed = pl.Squeezed()
     chunk_rows = CAP_OWNER * block_size + META_ROWS
     return pl.pallas_call(
-        diag_kernel,
+        functools.partial(diag_kernel, per_row),
         out_shape=jax.ShapeDtypeStruct((owner_count, chunk_rows, block_size), jnp.bfloat16),
         grid_spec=pltpu.PrefetchScalarGridSpec(
             num_scalar_prefetch=2,
@@ -132,17 +131,26 @@
     )(bucket, cols, *([a_blocks] * n_k), *([table] * (ROWS_PER_STEP * n_k)), prolong)
 
 
+REDUCE_CHUNK = 16
+
+
 def reduce_kernel(has_init, slot_ref, *refs):
     if has_init:
         init_ref, blocks_ref, out_ref = refs
-        out_ref[...] = init_ref[...]
     else:
         blocks_ref, out_ref = refs
-        out_ref[...] = jnp.zeros_like(out_ref)
+    step = pl.program_id(0)
     slot_count = out_ref.shape[0]
 
+    @pl.when(step == 0)
+    def _():
+        if has_init:
+            out_ref[...] = init_ref[...]
+        else:
+            out_ref[...] = jnp.zeros_like(out_ref)
+
     def add_block(index, carry):
-        slot = slot_ref[index]
+        slot = slot_ref[step * REDUCE_CHUNK + index]
 
         @pl.when((slot >= 0) & (slot < slot_count))
         def _():
@@ -151,24 +159,28 @@
 
         return carry
 
-    lax.fori_loop(0, blocks_ref.shape[0], add_block, 0)
+    lax.fori_loop(0, REDUCE_CHUNK, add_block, 0)
 
 
 def reduce_by_slot(slot_of_block, blocks, init=None):
     block_count, block_size, unused_size = blocks.shape
-    whole = lambda shape: pl.BlockSpec(shape, lambda i, s: (0,) * len(shape))
     out_shape = (CB_DEV, block_size, block_size)
-    in_specs = [whole(blocks.shape)]
+    whole = pl.BlockSpec(out_shape, lambda i, s: (0, 0, 0))
+    in_specs = [pl.BlockSpec((REDUCE_CHUNK, block_size, block_size), lambda i, s: (i, 0, 0))]
     operands = [blocks]
     if init is not None:
-        in_specs = [whole(out_shape)] + in_specs
+        in_specs = [whole] + in_specs
         operands = [init] + operands
     return pl.pallas_call(
         functools.partial(reduce_kernel, init is not None),
         out_shape=jax.ShapeDtypeStruct(out_shape, jnp.float32),
         grid_spec=pltpu.PrefetchScalarGridSpec(
-            num_scalar_prefetch=1, grid=(1,), in_specs=in_specs, out_specs=whole(out_shape)
-        ),
+            num_scalar_prefetch=1,
+            grid=(block_count // REDUCE_CHUNK,),
+            in_specs=in_specs,
+            out_specs=whole,
+        ),
+        compiler_params=pltpu.CompilerParams(dimension_semantics=("arbitrary",)),
         cost_estimate=pl.CostEstimate(
             flops=block_count * block_size * block_size,
             bytes_accessed=blocks.size * 2 + 8 * CB_DEV * block_size * block_size,

time: 202 us -> 203 us (level)
  no operation moved by 1% of the time
where the time goes in v8:
time: 203 us
  waiting for transfers between devices  135 us (67%)
  Pallas kernels  25.4 us (13%)
  starting transfers between devices  21.4 us (11%)
  between operations  13.4 us (7%)
  local copies, waits for them, and re-layouts  4.67 us (2%)
  other arithmetic  2.77 us (1%)
    all_to_all x1, waiting for transfers between devices, per_device(): lax.all_to_all(outgoing_off, 'wide', split_axis=0, concat_axis=0, tiled=T...  89.9 us
    all_gather x1, waiting for transfers between devices, per_device(): shard_blocks = lax.all_gather(prolong, 'narrow', axis=0, tiled=True)  42.7 us
    all_to_all x1, starting transfers between devices, per_device(): lax.all_to_all(outgoing_diag, 'wide', split_axis=0, concat_axis=0, tiled=...  13 us
    pallas_call x2, Pallas kernels, reduce_by_slot(): pl.pallas_call(functools.partial(reduce_kernel, init is not None), out_sh...  12.7 us
    all_to_all x1, starting transfers between devices, per_device(): lax.all_to_all(outgoing_off, 'wide', split_axis=0, concat_axis=0, tiled=T...  8.38 us
    pallas_call x1, Pallas kernels, galerkin_buckets(): pl.pallas_call(functools.partial(galerkin_kernel, n_k), out_shape=jax.Sha...  7.15 us
    pallas_call x1, Pallas kernels, diag_buckets(): pl.pallas_call(functools.partial(diag_kernel, per_row), out_shape=jax.Sha...  5.48 us
  transfers between devices with their start and end apart: 3, of which 3 were waited for; matrix products, arithmetic and copies ran while one was open for 4% of the time, Pallas kernels for 9%

profile of v8, /device:TPU:3, one launch (start us, length us, event | category | flops | bytes accessed | tf_op | source)
XLA Modules:
  0.0 202.6 jit_solution(14490570437829120854)
XLA Ops:
  6.5 0.0 all-gather.2.cloned.1.call-start
  6.5 0.7 all-gather.2.cloned.1.call-update
  7.3 1.4 copy.24.slot_ref
  8.6 0.9 convert_reduce_fusion
  9.5 1.2 add_clamp_fusion.bucket_ref
  10.8 5.5 %shard_map.55 = bf16[32,272,128]{2,1,0:T(8,128)(2,1)} custom-call(s32[16]{0:T(128)} %add_clamp_fusion.bucket_ref, s32[16,3]{1,0:T(8,128)} %copy.24.slot_ref, bf16[16,3,128,128]{3,2,1,0:T(8,128)(2,1)} %refs_1_.1, bf16[16,128,128]{2,1,0:T(8,128)(2,1)} %refs_10_.1), custom_call_target="tpu_custom_call" | custom-call | flops 134217728 | bytes 3276800 | tf_op jit(solution)/shard_map/pallas_call | solution.py:78
  16.2 0.0 copy-start
  16.2 13.0 %all-to-all-start = ((bf16[32,272,128]{2,1,0:T(8,128)(2,1)}), bf16[32,272,128]{2,1,0:T(8,128)(2,1)S(1)}, u32[]{:S(2)}, u32[]{:S(2)}) async-start(bf16[32,272,128]{2,1,0:T(8,128)(2,1)} %shard_map.55), calls=%async_computation | async-start | bytes 4456448 | tf_op jit(solution)/shard_map/all_to_all | solution.py:202
  29.3 0.0 copy-done
  29.3 0.1 copy.29
  29.4 0.6 broadcast_clamp_fusion.cols_ref
  30.0 42.7 %all-gather.2.cloned.1.call-done.refs_2_.refs_3_.refs_4_.refs_5_.refs_6_.refs_7_.refs_8_.refs_9_ = bf16[256,128,128]{2,1,0:T(8,128)(2,1)} async-done(((bf16[16,128,128]{2,1,0:T(8,128)(2,1)}), bf16[256,128,128]{2,1,0:T(8,128)(2,1)}) %all-gather.2.cloned.1.call-update) | async-done | bytes 8388624 | tf_op jit(solution)/shard_map/all_gather | solution.py:208
  72.7 7.1 %shard_map.57 = bf16[64,2,128,128]{3,2,1,0:T(8,128)(2,1)} custom-call(s32[16]{0:T(128)} %add_clamp_fusion.bucket_ref, s32[16,2]{1,0:T(8,128)} %broadcast_clamp_fusion.cols_ref, bf16[16,3,128,128]{3,2,1,0:T(8,128)(2,1)} %refs_1_.1, bf16[16,3,128,128]{3,2,1,0:T(8,128)(2,1)} %refs_1_.1, ...), custom_call_target="tpu_custom_call" | custom-call | flops 268435456 | bytes 6815744 | tf_op jit(solution)/shard_map/pallas_call | solution.py:120
  79.8 1.6 all-to-all-done
  81.5 8.4 %all-to-all-start.1 = ((bf16[32,4,128,128]{3,2,1,0:T(8,128)(2,1)}), bf16[32,4,128,128]{3,2,1,0:T(8,128)(2,1)}, u32[]{:S(2)}, u32[]{:S(2)}) async-start(bf16[32,4,128,128]{3,2,1,0:T(8,128)(2,1)} %bitcast.7), calls=%async_computation.1 | async-start | bytes 8388608 | tf_op jit(solution)/shard_map/all_to_all | solution.py:214
  89.9 0.1 copy.25
  90.0 0.1 copy.27
  90.1 0.6 reshape_squeeze.3.slot_ref
  90.7 0.1 copy.26
  90.8 0.7 reshape.21.slot_ref
  91.5 1.6 slice.23
  93.1 4.8 %shard_map.56.refs_0_ = f32[24,128,128]{2,1,0:T(8,128)} custom-call(s32[64]{0:T(128)} %reshape_squeeze.3.slot_ref, bf16[64,128,128]{2,1,0:T(8,128)(2,1)} %bitcast.8), custom_call_target="tpu_custom_call" | custom-call | flops 1048576 | bytes 5242880 | tf_op jit(solution)/shard_map/pallas_call | solution.py:174
  97.9 89.9 %all-to-all-done.1 = bf16[32,4,128,128]{3,2,1,0:T(8,128)(2,1)} async-done(((bf16[32,4,128,128]{3,2,1,0:T(8,128)(2,1)}), bf16[32,4,128,128]{3,2,1,0:T(8,128)(2,1)}, u32[]{:S(2)}, u32[]{:S(2)}) %all-to-all-start.1) | async-done | bytes 4194336 | tf_op jit(solution)/shard_map/all_to_all | solution.py:214
  187.8 7.9 %shard_map.58 = f32[24,128,128]{2,1,0:T(8,128)} custom-call(s32[128]{0:T(128)} %reshape.21.slot_ref, f32[24,128,128]{2,1,0:T(8,128)} %shard_map.56.refs_0_, bf16[128,128,128]{2,1,0:T(8,128)(2,1)} %bitcast.2.refs_1_), custom_call_target="tpu_custom_call" | custom-call | flops 2097152 | bytes 7340032 | tf_op jit(solution)/shard_map/pallas_call | solution.py:174
  (5 shorter events, 0.0 us)
Async XLA Ops:
  6.5 66.1 %all-gather.2.cloned.1.call-start = ((), (), s32[]{:S(2)}) async-start(), calls=%async_computation.2 | async-start | bytes 8912896 | tf_op jit(solution)/shard_map/all_gather | solution.py:208
  16.2 13.0 %copy-start = (s32[16,3]{0,1:T(4,128)S(1)}, s32[16,3]{0,1:T(4,128)}, u32[]{:S(2)}) copy-start(s32[16,3]{0,1:T(4,128)} %param.6) | copy-start | bytes 580
  16.2 65.2 %all-to-all-start = ((bf16[32,272,128]{2,1,0:T(8,128)(2,1)}), bf16[32,272,128]{2,1,0:T(8,128)(2,1)S(1)}, u32[]{:S(2)}, u32[]{:S(2)}) async-start(bf16[32,272,128]{2,1,0:T(8,128)(2,1)} %shard_map.55), calls=%async_computation | async-start | bytes 4456448 | tf_op jit(solution)/shard_map/all_to_all | solution.py:202
  81.5 106.3 %all-to-all-start.1 = ((bf16[32,4,128,128]{3,2,1,0:T(8,128)(2,1)}), bf16[32,4,128,128]{3,2,1,0:T(8,128)(2,1)}, u32[]{:S(2)}, u32[]{:S(2)}) async-start(bf16[32,4,128,128]{3,2,1,0:T(8,128)(2,1)} %bitcast.7), calls=%async_computation.1 | async-start | bytes 8388608 | tf_op jit(solution)/shard_map/all_to_all | solution.py:214
Sparse Core Ops, SparseCore 0:
  9.4 63.1 all-gather.1

commit v9 on v7

--- a/solution.py
+++ b/solution.py
@@ -11,7 +11,7 @@
 CB_DEV = 24
 
 
-ROWS_PER_STEP = 4
+ROWS_PER_STEP = 8
 
 
 def galerkin_kernel(n_k, bucket_ref, cols_ref, *refs):
@@ -132,26 +132,38 @@
     )(bucket, cols, *([a_blocks] * n_k), *([table] * (ROWS_PER_STEP * n_k)), prolong)
 
 
+ACCUMULATORS = 4
+
+
 def reduce_kernel(has_init, slot_ref, *refs):
     if has_init:
-        init_ref, blocks_ref, out_ref = refs
-        out_ref[...] = init_ref[...]
+        init_ref, blocks_ref, out_ref = refs[:3]
     else:
-        blocks_ref, out_ref = refs
-        out_ref[...] = jnp.zeros_like(out_ref)
+        blocks_ref, out_ref = refs[:2]
+    acc_refs = refs[-ACCUMULATORS:]
     slot_count = out_ref.shape[0]
-
-    def add_block(index, carry):
-        slot = slot_ref[index]
-
-        @pl.when((slot >= 0) & (slot < slot_count))
-        def _():
-            target = jnp.clip(slot, 0, slot_count - 1)
-            out_ref[target] = out_ref[target] + blocks_ref[index].astype(jnp.float32)
+    for acc_ref in acc_refs:
+        acc_ref[...] = jnp.zeros_like(acc_ref)
+
+    def add_blocks(index, carry):
+        for j, acc_ref in enumerate(acc_refs):
+            block = index * ACCUMULATORS + j
+            slot = slot_ref[block]
+
+            @pl.when((slot >= 0) & (slot < slot_count))
+            def _():
+                target = jnp.clip(slot, 0, slot_count - 1)
+                acc_ref[target] = acc_ref[target] + blocks_ref[block].astype(jnp.float32)
 
         return carry
 
-    lax.fori_loop(0, blocks_ref.shape[0], add_block, 0)
+    lax.fori_loop(0, blocks_ref.shape[0] // ACCUMULATORS, add_blocks, 0)
+    total = acc_refs[0][...]
+    for acc_ref in acc_refs[1:]:
+        total = total + acc_ref[...]
+    if has_init:
+        total = total + init_ref[...]
+    out_ref[...] = total
 
 
 def reduce_by_slot(slot_of_block, blocks, init=None):
@@ -167,7 +179,11 @@
         functools.partial(reduce_kernel, init is not None),
         out_shape=jax.ShapeDtypeStruct(out_shape, jnp.float32),
         grid_spec=pltpu.PrefetchScalarGridSpec(
-            num_scalar_prefetch=1, grid=(1,), in_specs=in_specs, out_specs=whole(out_shape)
+            num_scalar_prefetch=1,
+            grid=(1,),
+            in_specs=in_specs,
+            out_specs=whole(out_shape),
+            scratch_shapes=[pltpu.VMEM(out_shape, jnp.float32)] * ACCUMULATORS,
         ),
         cost_estimate=pl.CostEstimate(
             flops=block_count * block_size * block_size,

time: 202 us -> 201 us (level)
  the two profiles are of different devices: /device:TPU:3 before, /device:TPU:7 now
where the time goes in v9:
time: 201 us; the launch traced here: 197 us
  waiting for transfers between devices  133 us (66%)
  Pallas kernels  22.2 us (11%)
  starting transfers between devices  20.6 us (10%)
  between operations  13.4 us (7%)
  local copies, waits for them, and re-layouts  4.67 us (2%)
  other arithmetic  2.77 us (1%)
    all_to_all x1, waiting for transfers between devices, per_device(): lax.all_to_all(outgoing_off, 'wide', split_axis=0, concat_axis=0, tiled=T...  86.4 us
    all_gather x1, waiting for transfers between devices, per_device(): shard_blocks = lax.all_gather(prolong, 'narrow', axis=0, tiled=True)  43.8 us
    all_to_all x1, starting transfers between devices, per_device(): lax.all_to_all(outgoing_diag, 'wide', split_axis=0, concat_axis=0, tiled=...  13 us
    pallas_call x2, Pallas kernels, reduce_by_slot(): pl.pallas_call(functools.partial(reduce_kernel, init is not None), out_sh...  11.8 us
    all_to_all x1, starting transfers between devices, per_device(): lax.all_to_all(outgoing_off, 'wide', split_axis=0, concat_axis=0, tiled=T...  7.61 us
    pallas_call x1, Pallas kernels, galerkin_buckets(): pl.pallas_call(functools.partial(galerkin_kernel, n_k), out_shape=jax.Sha...  6.12 us
    pallas_call x1, Pallas kernels, diag_buckets(): pl.pallas_call(diag_kernel, out_shape=jax.ShapeDtypeStruct((owner_count,...  4.33 us
  transfers between devices with their start and end apart: 3, of which 3 were waited for; matrix products, arithmetic and copies ran while one was open for 4% of the time, Pallas kernels for 8%

profile of v9, /device:TPU:7, one launch (start us, length us, event | category | flops | bytes accessed | tf_op | source)
XLA Modules:
  0.0 197.0 jit_solution(16771757202860715649)
XLA Ops:
  6.5 0.0 all-gather.2.cloned.1.call-start
  6.5 0.7 all-gather.2.cloned.1.call-update
  7.3 1.4 copy.24.slot_ref
  8.6 0.9 convert_reduce_fusion
  9.5 1.2 add_clamp_fusion.bucket_ref
  10.8 4.3 %shard_map.55 = bf16[32,272,128]{2,1,0:T(8,128)(2,1)} custom-call(s32[16]{0:T(128)} %add_clamp_fusion.bucket_ref, s32[16,3]{1,0:T(8,128)} %copy.24.slot_ref, bf16[16,3,128,128]{3,2,1,0:T(8,128)(2,1)} %refs_1_.1, bf16[16,128,128]{2,1,0:T(8,128)(2,1)} %refs_18_.1), custom_call_target="tpu_custom_call" | custom-call | flops 134217728 | bytes 3276800 | tf_op jit(solution)/shard_map/pallas_call | solution.py:79
  15.1 0.0 copy-start
  15.1 13.0 %all-to-all-start = ((bf16[32,272,128]{2,1,0:T(8,128)(2,1)}), bf16[32,272,128]{2,1,0:T(8,128)(2,1)S(1)}, u32[]{:S(2)}, u32[]{:S(2)}) async-start(bf16[32,272,128]{2,1,0:T(8,128)(2,1)} %shard_map.55), calls=%async_computation | async-start | bytes 4456448 | tf_op jit(solution)/shard_map/all_to_all | solution.py:206
  28.1 0.0 copy-done
  28.1 0.1 copy.29
  28.2 0.6 broadcast_clamp_fusion.cols_ref
  28.8 43.8 %all-gather.2.cloned.1.call-done.refs_2_.refs_3_.refs_4_.refs_5_.refs_6_.refs_7_.refs_8_.refs_9_.refs_10_.refs_11_.refs_12_.refs_13_.refs_14_.refs_15_.refs_16_.refs_17_ = bf16[256,128,128]{2,1,0:T(8,128)(2,1)} async-done(((bf16[16,128,128]{2,1,0:T(8,128)(2,1)}), bf16[256,128,128]{2,1,0:T(8,128)(2,1)}) %all-gather.2.cloned.1.call-update) | async-done | bytes 8388624 | tf_op jit(solution)/shard_map/all_gather | solution.py:212
  72.6 6.1 %shard_map.57 = bf16[64,2,128,128]{3,2,1,0:T(8,128)(2,1)} custom-call(s32[16]{0:T(128)} %add_clamp_fusion.bucket_ref, s32[16,2]{1,0:T(8,128)} %broadcast_clamp_fusion.cols_ref, bf16[16,3,128,128]{3,2,1,0:T(8,128)(2,1)} %refs_1_.1, bf16[16,3,128,128]{3,2,1,0:T(8,128)(2,1)} %refs_1_.1, ...), custom_call_target="tpu_custom_call" | custom-call | flops 268435456 | bytes 6815744 | tf_op jit(solution)/shard_map/pallas_call | solution.py:121
  78.8 2.4 %all-to-all-done = bf16[32,272,128]{2,1,0:T(8,128)(2,1)S(1)} async-done(((bf16[32,272,128]{2,1,0:T(8,128)(2,1)}), bf16[32,272,128]{2,1,0:T(8,128)(2,1)S(1)}, u32[]{:S(2)}, u32[]{:S(2)}) %all-to-all-start) | async-done | bytes 2228256 | tf_op jit(solution)/shard_map/all_to_all | solution.py:206
  81.2 7.6 %all-to-all-start.1 = ((bf16[32,4,128,128]{3,2,1,0:T(8,128)(2,1)}), bf16[32,4,128,128]{3,2,1,0:T(8,128)(2,1)}, u32[]{:S(2)}, u32[]{:S(2)}) async-start(bf16[32,4,128,128]{3,2,1,0:T(8,128)(2,1)} %bitcast.7), calls=%async_computation.1 | async-start | bytes 8388608 | tf_op jit(solution)/shard_map/all_to_all | solution.py:218
  88.8 0.1 copy.25
  88.9 0.1 copy.27
  89.0 0.6 reshape_squeeze.3.slot_ref
  89.6 0.1 copy.26
  89.7 0.7 reshape.21.slot_ref
  90.5 1.6 slice.23
  92.0 4.9 %shard_map.56.refs_0_ = f32[24,128,128]{2,1,0:T(8,128)} custom-call(s32[64]{0:T(128)} %reshape_squeeze.3.slot_ref, bf16[64,128,128]{2,1,0:T(8,128)(2,1)} %bitcast.8), custom_call_target="tpu_custom_call" | custom-call | flops 1048576 | bytes 5242880 | tf_op jit(solution)/shard_map/pallas_call | solution.py:178
  96.9 86.4 %all-to-all-done.1 = bf16[32,4,128,128]{3,2,1,0:T(8,128)(2,1)} async-done(((bf16[32,4,128,128]{3,2,1,0:T(8,128)(2,1)}), bf16[32,4,128,128]{3,2,1,0:T(8,128)(2,1)}, u32[]{:S(2)}, u32[]{:S(2)}) %all-to-all-start.1) | async-done | bytes 4194336 | tf_op jit(solution)/shard_map/all_to_all | solution.py:218
  183.3 6.9 %shard_map.58 = f32[24,128,128]{2,1,0:T(8,128)} custom-call(s32[128]{0:T(128)} %reshape.21.slot_ref, f32[24,128,128]{2,1,0:T(8,128)} %shard_map.56.refs_0_, bf16[128,128,128]{2,1,0:T(8,128)(2,1)} %bitcast.2.refs_1_), custom_call_target="tpu_custom_call" | custom-call | flops 2097152 | bytes 7340032 | tf_op jit(solution)/shard_map/pallas_call | solution.py:178
  (5 shorter events, 0.0 us)
Async XLA Ops:
  6.5 66.1 %all-gather.2.cloned.1.call-start = ((), (), s32[]{:S(2)}) async-start(), calls=%async_computation.2 | async-start | bytes 8912896 | tf_op jit(solution)/shard_map/all_gather | solution.py:212
  15.1 13.0 %copy-start = (s32[16,3]{0,1:T(4,128)S(1)}, s32[16,3]{0,1:T(4,128)}, u32[]{:S(2)}) copy-start(s32[16,3]{0,1:T(4,128)} %param.6) | copy-start | bytes 580
  15.1 66.1 %all-to-all-start = ((bf16[32,272,128]{2,1,0:T(8,128)(2,1)}), bf16[32,272,128]{2,1,0:T(8,128)(2,1)S(1)}, u32[]{:S(2)}, u32[]{:S(2)}) async-start(bf16[32,272,128]{2,1,0:T(8,128)(2,1)} %shard_map.55), calls=%async_computation | async-start | bytes 4456448 | tf_op jit(solution)/shard_map/all_to_all | solution.py:206
  81.2 102.2 %all-to-all-start.1 = ((bf16[32,4,128,128]{3,2,1,0:T(8,128)(2,1)}), bf16[32,4,128,128]{3,2,1,0:T(8,128)(2,1)}, u32[]{:S(2)}, u32[]{:S(2)}) async-start(bf16[32,4,128,128]{3,2,1,0:T(8,128)(2,1)} %bitcast.7), calls=%async_computation.1 | async-start | bytes 8388608 | tf_op jit(solution)/shard_map/all_to_all | solution.py:218
Sparse Core Ops, SparseCore 0:
  9.4 63.1 all-gather.1

commit v10 on v9

--- a/solution.py
+++ b/solution.py
@@ -149,15 +149,13 @@
         for j, acc_ref in enumerate(acc_refs):
             block = index * ACCUMULATORS + j
             slot = slot_ref[block]
-
-            @pl.when((slot >= 0) & (slot < slot_count))
-            def _():
-                target = jnp.clip(slot, 0, slot_count - 1)
-                acc_ref[target] = acc_ref[target] + blocks_ref[block].astype(jnp.float32)
-
+            valid = (slot >= 0) & (slot < slot_count)
+            target = jnp.clip(slot, 0, slot_count - 1)
+            addend = jnp.where(valid, blocks_ref[block].astype(jnp.float32), 0.0)
+            acc_ref[target] = acc_ref[target] + addend
         return carry
 
-    lax.fori_loop(0, blocks_ref.shape[0] // ACCUMULATORS, add_blocks, 0)
+    lax.fori_loop(0, blocks_ref.shape[0] // ACCUMULATORS, add_blocks, 0, unroll=4)
     total = acc_refs[0][...]
     for acc_ref in acc_refs[1:]:
         total = total + acc_ref[...]

time: 201 us -> 200 us (level)
  no operation moved by 1% of the time
where the time goes in v10:
time: 200 us; the launch traced here: 196 us
  waiting for transfers between devices  134 us (67%)
  Pallas kernels  21.1 us (11%)
  starting transfers between devices  20.6 us (10%)
  between operations  13.4 us (7%)
  local copies, waits for them, and re-layouts  4.67 us (2%)
  other arithmetic  2.77 us (1%)
    all_to_all x1, waiting for transfers between devices, per_device(): lax.all_to_all(outgoing_off, 'wide', split_axis=0, concat_axis=0, tiled=T...  86.8 us
    all_gather x1, waiting for transfers between devices, per_device(): shard_blocks = lax.all_gather(prolong, 'narrow', axis=0, tiled=True)  43.8 us
    all_to_all x1, starting transfers between devices, per_device(): lax.all_to_all(outgoing_diag, 'wide', split_axis=0, concat_axis=0, tiled=...  13 us
    pallas_call x2, Pallas kernels, reduce_by_slot(): pl.pallas_call(functools.partial(reduce_kernel, init is not None), out_sh...  10.6 us
    all_to_all x1, starting transfers between devices, per_device(): lax.all_to_all(outgoing_off, 'wide', split_axis=0, concat_axis=0, tiled=T...  7.62 us
    pallas_call x1, Pallas kernels, galerkin_buckets(): pl.pallas_call(functools.partial(galerkin_kernel, n_k), out_shape=jax.Sha...  6.12 us
    pallas_call x1, Pallas kernels, diag_buckets(): pl.pallas_call(diag_kernel, out_shape=jax.ShapeDtypeStruct((owner_count,...  4.33 us
  transfers between devices with their start and end apart: 3, of which 3 were waited for; matrix products, arithmetic and copies ran while one was open for 4% of the time, Pallas kernels for 8%

profile of v10, /device:TPU:7, one launch (start us, length us, event | category | flops | bytes accessed | tf_op | source)
XLA Modules:
  0.0 196.3 jit_solution(6234384426532654196)
XLA Ops:
  6.5 0.0 all-gather.2.cloned.1.call-start
  6.5 0.7 all-gather.2.cloned.1.call-update
  7.3 1.4 copy.24.slot_ref
  8.6 0.9 convert_reduce_fusion
  9.5 1.2 add_clamp_fusion.bucket_ref
  10.8 4.3 %shard_map.55 = bf16[32,272,128]{2,1,0:T(8,128)(2,1)} custom-call(s32[16]{0:T(128)} %add_clamp_fusion.bucket_ref, s32[16,3]{1,0:T(8,128)} %copy.24.slot_ref, bf16[16,3,128,128]{3,2,1,0:T(8,128)(2,1)} %refs_1_.1, bf16[16,128,128]{2,1,0:T(8,128)(2,1)} %refs_18_.1), custom_call_target="tpu_custom_call" | custom-call | flops 134217728 | bytes 3276800 | tf_op jit(solution)/shard_map/pallas_call | solution.py:79
  15.1 0.0 copy-start
  15.1 13.0 %all-to-all-start = ((bf16[32,272,128]{2,1,0:T(8,128)(2,1)}), bf16[32,272,128]{2,1,0:T(8,128)(2,1)S(1)}, u32[]{:S(2)}, u32[]{:S(2)}) async-start(bf16[32,272,128]{2,1,0:T(8,128)(2,1)} %shard_map.55), calls=%async_computation | async-start | bytes 4456448 | tf_op jit(solution)/shard_map/all_to_all | solution.py:204
  28.1 0.0 copy-done
  28.1 0.1 copy.29
  28.2 0.6 broadcast_clamp_fusion.cols_ref
  28.8 43.8 %all-gather.2.cloned.1.call-done.refs_2_.refs_3_.refs_4_.refs_5_.refs_6_.refs_7_.refs_8_.refs_9_.refs_10_.refs_11_.refs_12_.refs_13_.refs_14_.refs_15_.refs_16_.refs_17_ = bf16[256,128,128]{2,1,0:T(8,128)(2,1)} async-done(((bf16[16,128,128]{2,1,0:T(8,128)(2,1)}), bf16[256,128,128]{2,1,0:T(8,128)(2,1)}) %all-gather.2.cloned.1.call-update) | async-done | bytes 8388624 | tf_op jit(solution)/shard_map/all_gather | solution.py:210
  72.6 6.1 %shard_map.57 = bf16[64,2,128,128]{3,2,1,0:T(8,128)(2,1)} custom-call(s32[16]{0:T(128)} %add_clamp_fusion.bucket_ref, s32[16,2]{1,0:T(8,128)} %broadcast_clamp_fusion.cols_ref, bf16[16,3,128,128]{3,2,1,0:T(8,128)(2,1)} %refs_1_.1, bf16[16,3,128,128]{3,2,1,0:T(8,128)(2,1)} %refs_1_.1, ...), custom_call_target="tpu_custom_call" | custom-call | flops 268435456 | bytes 6815744 | tf_op jit(solution)/shard_map/pallas_call | solution.py:121
  78.8 2.4 %all-to-all-done = bf16[32,272,128]{2,1,0:T(8,128)(2,1)S(1)} async-done(((bf16[32,272,128]{2,1,0:T(8,128)(2,1)}), bf16[32,272,128]{2,1,0:T(8,128)(2,1)S(1)}, u32[]{:S(2)}, u32[]{:S(2)}) %all-to-all-start) | async-done | bytes 2228256 | tf_op jit(solution)/shard_map/all_to_all | solution.py:204
  81.2 7.6 %all-to-all-start.1 = ((bf16[32,4,128,128]{3,2,1,0:T(8,128)(2,1)}), bf16[32,4,128,128]{3,2,1,0:T(8,128)(2,1)}, u32[]{:S(2)}, u32[]{:S(2)}) async-start(bf16[32,4,128,128]{3,2,1,0:T(8,128)(2,1)} %bitcast.7), calls=%async_computation.1 | async-start | bytes 8388608 | tf_op jit(solution)/shard_map/all_to_all | solution.py:216
  88.8 0.1 copy.25
  88.9 0.1 copy.27
  89.0 0.6 reshape_squeeze.3.slot_ref
  89.6 0.1 copy.26
  89.7 0.7 reshape.21.slot_ref
  90.5 1.6 slice.23
  92.0 4.5 %shard_map.56.refs_0_ = f32[24,128,128]{2,1,0:T(8,128)} custom-call(s32[64]{0:T(128)} %reshape_squeeze.3.slot_ref, bf16[64,128,128]{2,1,0:T(8,128)(2,1)} %bitcast.8), custom_call_target="tpu_custom_call" | custom-call | flops 1048576 | bytes 5242880 | tf_op jit(solution)/shard_map/pallas_call | solution.py:176
  96.6 86.8 %all-to-all-done.1 = bf16[32,4,128,128]{3,2,1,0:T(8,128)(2,1)} async-done(((bf16[32,4,128,128]{3,2,1,0:T(8,128)(2,1)}), bf16[32,4,128,128]{3,2,1,0:T(8,128)(2,1)}, u32[]{:S(2)}, u32[]{:S(2)}) %all-to-all-start.1) | async-done | bytes 4194336 | tf_op jit(solution)/shard_map/all_to_all | solution.py:216
  183.3 6.1 %shard_map.58 = f32[24,128,128]{2,1,0:T(8,128)} custom-call(s32[128]{0:T(128)} %reshape.21.slot_ref, f32[24,128,128]{2,1,0:T(8,128)} %shard_map.56.refs_0_, bf16[128,128,128]{2,1,0:T(8,128)(2,1)} %bitcast.2.refs_1_), custom_call_target="tpu_custom_call" | custom-call | flops 2097152 | bytes 7340032 | tf_op jit(solution)/shard_map/pallas_call | solution.py:176
  (5 shorter events, 0.0 us)
Async XLA Ops:
  6.5 66.1 %all-gather.2.cloned.1.call-start = ((), (), s32[]{:S(2)}) async-start(), calls=%async_computation.2 | async-start | bytes 8912896 | tf_op jit(solution)/shard_map/all_gather | solution.py:210
  15.1 13.0 %copy-start = (s32[16,3]{0,1:T(4,128)S(1)}, s32[16,3]{0,1:T(4,128)}, u32[]{:S(2)}) copy-start(s32[16,3]{0,1:T(4,128)} %param.6) | copy-start | bytes 580
  15.1 66.1 %all-to-all-start = ((bf16[32,272,128]{2,1,0:T(8,128)(2,1)}), bf16[32,272,128]{2,1,0:T(8,128)(2,1)S(1)}, u32[]{:S(2)}, u32[]{:S(2)}) async-start(bf16[32,272,128]{2,1,0:T(8,128)(2,1)} %shard_map.55), calls=%async_computation | async-start | bytes 4456448 | tf_op jit(solution)/shard_map/all_to_all | solution.py:204
  81.2 102.2 %all-to-all-start.1 = ((bf16[32,4,128,128]{3,2,1,0:T(8,128)(2,1)}), bf16[32,4,128,128]{3,2,1,0:T(8,128)(2,1)}, u32[]{:S(2)}, u32[]{:S(2)}) async-start(bf16[32,4,128,128]{3,2,1,0:T(8,128)(2,1)} %bitcast.7), calls=%async_computation.1 | async-start | bytes 8388608 | tf_op jit(solution)/shard_map/all_to_all | solution.py:216
Sparse Core Ops, SparseCore 0:
  9.4 63.1 all-gather.1

commit v11 on v10

--- a/solution.py
+++ b/solution.py
@@ -11,7 +11,7 @@
 CB_DEV = 24
 
 
-ROWS_PER_STEP = 8
+ROWS_PER_STEP = 16
 
 
 def galerkin_kernel(n_k, bucket_ref, cols_ref, *refs):

time: 200 us -> 200 us (level)
  transfers between devices with their start and end apart: 3 -> 3, of which waited for: 3 -> 3; matrix products, arithmetic and copies ran while one was open for 4% -> 4% of each run, Pallas kernels for 8% -> 7%
where the time goes in v11:
time: 200 us; the launch traced here: 196 us
  waiting for transfers between devices  134 us (67%)
  Pallas kernels  20.6 us (10%)
  starting transfers between devices  20.5 us (10%)
  between operations  13.4 us (7%)
  local copies, waits for them, and re-layouts  4.67 us (2%)
  other arithmetic  2.77 us (1%)
    all_to_all x1, waiting for transfers between devices, per_device(): lax.all_to_all(outgoing_off, 'wide', split_axis=0, concat_axis=0, tiled=T...  86.7 us
    all_gather x1, waiting for transfers between devices, per_device(): shard_blocks = lax.all_gather(prolong, 'narrow', axis=0, tiled=True)  44 us
    all_to_all x1, starting transfers between devices, per_device(): lax.all_to_all(outgoing_diag, 'wide', split_axis=0, concat_axis=0, tiled=...  13 us
    pallas_call x2, Pallas kernels, reduce_by_slot(): pl.pallas_call(functools.partial(reduce_kernel, init is not None), out_sh...  10.6 us
    all_to_all x1, starting transfers between devices, per_device(): lax.all_to_all(outgoing_off, 'wide', split_axis=0, concat_axis=0, tiled=T...  7.47 us
    pallas_call x1, Pallas kernels, galerkin_buckets(): pl.pallas_call(functools.partial(galerkin_kernel, n_k), out_shape=jax.Sha...  5.81 us
    pallas_call x1, Pallas kernels, diag_buckets(): pl.pallas_call(diag_kernel, out_shape=jax.ShapeDtypeStruct((owner_count,...  4.16 us
  transfers between devices with their start and end apart: 3, of which 3 were waited for; matrix products, arithmetic and copies ran while one was open for 4% of the time, Pallas kernels for 7%

profile of v11, /device:TPU:7, one launch (start us, length us, event | category | flops | bytes accessed | tf_op | source)
XLA Modules:
  0.0 195.9 jit_solution(9780013414767670744)
XLA Ops:
  6.5 0.0 all-gather.2.cloned.1.call-start
  6.5 0.7 all-gather.2.cloned.1.call-update
  7.3 1.4 copy.24.slot_ref
  8.6 0.9 convert_reduce_fusion
  9.5 1.2 add_clamp_fusion.bucket_ref
  10.8 4.2 %shard_map.55 = bf16[32,272,128]{2,1,0:T(8,128)(2,1)} custom-call(s32[16]{0:T(128)} %add_clamp_fusion.bucket_ref, s32[16,3]{1,0:T(8,128)} %copy.24.slot_ref, bf16[16,3,128,128]{3,2,1,0:T(8,128)(2,1)} %refs_1_.1, bf16[16,128,128]{2,1,0:T(8,128)(2,1)} %refs_34_.1), custom_call_target="tpu_custom_call" | custom-call | flops 134217728 | bytes 3276800 | tf_op jit(solution)/shard_map/pallas_call | solution.py:79
  14.9 0.0 copy-start
  14.9 13.0 %all-to-all-start = ((bf16[32,272,128]{2,1,0:T(8,128)(2,1)}), bf16[32,272,128]{2,1,0:T(8,128)(2,1)S(1)}, u32[]{:S(2)}, u32[]{:S(2)}) async-start(bf16[32,272,128]{2,1,0:T(8,128)(2,1)} %shard_map.55), calls=%async_computation | async-start | bytes 4456448 | tf_op jit(solution)/shard_map/all_to_all | solution.py:204
  27.9 0.0 copy-done
  27.9 0.1 copy.29
  28.0 0.6 broadcast_clamp_fusion.cols_ref
  28.6 44.0 %all-gather.2.cloned.1.call-done.refs_2_.refs_3_.refs_4_.refs_5_.refs_6_.refs_7_.refs_8_.refs_9_.refs_10_.refs_11_.refs_12_.refs_13_.refs_14_.refs_15_.refs_16_.refs_17_.refs_18_.refs_19_.refs_20_.refs_21_.refs_22_.refs_23_.refs_24_.refs_25_.refs_26_.refs_27_.refs_28_.refs_29_.refs_30_.refs_31_.refs_32_.refs_33_ = bf16[256,128,128]{2,1,0:T(8,128)(2,1)} async-done(((bf16[16,128,128]{2,1,0:T(8,128)(2,1)}), ...) | async-done | bytes 8388624 | tf_op jit(solution)/shard_map/all_gather | solution.py:210
  72.6 5.8 %shard_map.57 = bf16[64,2,128,128]{3,2,1,0:T(8,128)(2,1)} custom-call(s32[16]{0:T(128)} %add_clamp_fusion.bucket_ref, s32[16,2]{1,0:T(8,128)} %broadcast_clamp_fusion.cols_ref, bf16[16,3,128,128]{3,2,1,0:T(8,128)(2,1)} %refs_1_.1, bf16[16,3,128,128]{3,2,1,0:T(8,128)(2,1)} %refs_1_.1, ...), custom_call_target="tpu_custom_call" | custom-call | flops 268435456 | bytes 6815744 | tf_op jit(solution)/shard_map/pallas_call | solution.py:121
  78.4 2.5 %all-to-all-done = bf16[32,272,128]{2,1,0:T(8,128)(2,1)S(1)} async-done(((bf16[32,272,128]{2,1,0:T(8,128)(2,1)}), bf16[32,272,128]{2,1,0:T(8,128)(2,1)S(1)}, u32[]{:S(2)}, u32[]{:S(2)}) %all-to-all-start) | async-done | bytes 2228256 | tf_op jit(solution)/shard_map/all_to_all | solution.py:204
  81.0 7.5 %all-to-all-start.1 = ((bf16[32,4,128,128]{3,2,1,0:T(8,128)(2,1)}), bf16[32,4,128,128]{3,2,1,0:T(8,128)(2,1)}, u32[]{:S(2)}, u32[]{:S(2)}) async-start(bf16[32,4,128,128]{3,2,1,0:T(8,128)(2,1)} %bitcast.7), calls=%async_computation.1 | async-start | bytes 8388608 | tf_op jit(solution)/shard_map/all_to_all | solution.py:216
  88.5 0.1 copy.25
  88.6 0.1 copy.27
  88.7 0.6 reshape_squeeze.3.slot_ref
  89.3 0.1 copy.26
  89.4 0.7 reshape.21.slot_ref
  90.1 1.6 slice.23
  91.7 4.5 %shard_map.56.refs_0_ = f32[24,128,128]{2,1,0:T(8,128)} custom-call(s32[64]{0:T(128)} %reshape_squeeze.3.slot_ref, bf16[64,128,128]{2,1,0:T(8,128)(2,1)} %bitcast.8), custom_call_target="tpu_custom_call" | custom-call | flops 1048576 | bytes 5242880 | tf_op jit(solution)/shard_map/pallas_call | solution.py:176
  96.2 86.7 %all-to-all-done.1 = bf16[32,4,128,128]{3,2,1,0:T(8,128)(2,1)} async-done(((bf16[32,4,128,128]{3,2,1,0:T(8,128)(2,1)}), bf16[32,4,128,128]{3,2,1,0:T(8,128)(2,1)}, u32[]{:S(2)}, u32[]{:S(2)}) %all-to-all-start.1) | async-done | bytes 4194336 | tf_op jit(solution)/shard_map/all_to_all | solution.py:216
  183.0 6.1 %shard_map.58 = f32[24,128,128]{2,1,0:T(8,128)} custom-call(s32[128]{0:T(128)} %reshape.21.slot_ref, f32[24,128,128]{2,1,0:T(8,128)} %shard_map.56.refs_0_, bf16[128,128,128]{2,1,0:T(8,128)(2,1)} %bitcast.2.refs_1_), custom_call_target="tpu_custom_call" | custom-call | flops 2097152 | bytes 7340032 | tf_op jit(solution)/shard_map/pallas_call | solution.py:176
  (5 shorter events, 0.0 us)
Async XLA Ops:
  6.5 66.1 %all-gather.2.cloned.1.call-start = ((), (), s32[]{:S(2)}) async-start(), calls=%async_computation.2 | async-start | bytes 8912896 | tf_op jit(solution)/shard_map/all_gather | solution.py:210
  14.9 13.0 %copy-start = (s32[16,3]{0,1:T(4,128)S(1)}, s32[16,3]{0,1:T(4,128)}, u32[]{:S(2)}) copy-start(s32[16,3]{0,1:T(4,128)} %param.6) | copy-start | bytes 580
  14.9 66.1 %all-to-all-start = ((bf16[32,272,128]{2,1,0:T(8,128)(2,1)}), bf16[32,272,128]{2,1,0:T(8,128)(2,1)S(1)}, u32[]{:S(2)}, u32[]{:S(2)}) async-start(bf16[32,272,128]{2,1,0:T(8,128)(2,1)} %shard_map.55), calls=%async_computation | async-start | bytes 4456448 | tf_op jit(solution)/shard_map/all_to_all | solution.py:204
  81.0 102.0 %all-to-all-start.1 = ((bf16[32,4,128,128]{3,2,1,0:T(8,128)(2,1)}), bf16[32,4,128,128]{3,2,1,0:T(8,128)(2,1)}, u32[]{:S(2)}, u32[]{:S(2)}) async-start(bf16[32,4,128,128]{3,2,1,0:T(8,128)(2,1)} %bitcast.7), calls=%async_computation.1 | async-start | bytes 8388608 | tf_op jit(solution)/shard_map/all_to_all | solution.py:216
Sparse Core Ops, SparseCore 0:
  9.4 63.1 all-gather.1

commit v12 on v11

--- a/solution.py
+++ b/solution.py
@@ -40,7 +40,7 @@
 META_ROWS = 16
 
 
-def diag_kernel(bucket_ref, slot_ref, a_ref, p_ref, out_ref):
+def diag_kernel(owner_ref, slot_ref, a_ref, p_ref, out_ref):
     step = pl.program_id(0)
     block_size = p_ref.shape[-1]
     per_row = slot_ref.shape[1]
@@ -53,7 +53,11 @@
     cols = lax.broadcasted_iota(jnp.int32, (META_ROWS, block_size), 1)
     for i in range(ROWS_PER_STEP):
         row = step * ROWS_PER_STEP + i
-        bucket = bucket_ref[row]
+        owner = owner_ref[row]
+        pos = jnp.int32(0)
+        for j in range(owner_ref.shape[0]):
+            pos = pos + jnp.where((j < row) & (owner_ref[j] == owner), 1, 0).astype(jnp.int32)
+        bucket = jnp.clip(owner * CAP_OWNER + pos, 0, out_ref.shape[0] * CAP_OWNER - 1)
         owner = bucket // CAP_OWNER
         pos = bucket - owner * CAP_OWNER
         product = jnp.dot(a_ref[i], p_ref[i], preferred_element_type=jnp.float32).astype(jnp.bfloat16)
@@ -72,7 +76,7 @@
         ).astype(jnp.bfloat16)
 
 
-def diag_buckets(a_blocks, prolong, slots, bucket, owner_count):
+def diag_buckets(a_blocks, prolong, slots, owners, owner_count):
     slab_rows, per_row, block_size, unused_size = a_blocks.shape
     squeezed = pl.Squeezed()
     chunk_rows = CAP_OWNER * block_size + META_ROWS
@@ -94,7 +98,7 @@
             bytes_accessed=2 * block_size * (2 * slab_rows * block_size + owner_count * chunk_rows),
             transcendentals=0,
         ),
-    )(bucket, slots.astype(jnp.int32), a_blocks, prolong)
+    )(owners.astype(jnp.int32), slots.astype(jnp.int32), a_blocks, prolong)
 
 
 def galerkin_buckets(a_blocks, ks, table, cols, prolong, bucket, bucket_count):
@@ -200,7 +204,7 @@
     same_owner = (owners[:, None] == owners[None, :]) & (row_ids[None, :] < row_ids[:, None])
     owner_position = jnp.sum(same_owner.astype(jnp.int32), axis=1)
     bucket = jnp.clip(owners * CAP_OWNER + owner_position, 0, bucket_count - 1).astype(jnp.int32)
-    outgoing_diag = diag_buckets(a_blocks, prolong, slots, bucket, owner_count)
+    outgoing_diag = diag_buckets(a_blocks, prolong, slots, owners, owner_count)
     arrived_diag = lax.all_to_all(outgoing_diag, "wide", split_axis=0, concat_axis=0, tiled=True)
     arrived_meta = arrived_diag[:, CAP_OWNER * block_size, : CAP_OWNER * per_row].astype(jnp.float32)
     arrived_slots = (jnp.round(arrived_meta).astype(jnp.int32) - 1).reshape(

time: 200 us -> 200 us (level)
  starting transfers between devices: 20.5 us -> 22.6 us
    all_to_all x1, waiting for transfers between devices: 2.54 us -> 0.4 us  [per_device(): lax.all_to_all(outgoing_diag, 'wide', split_axis=0, concat_axis=0, tiled=...]
    all_to_all x1, starting transfers between devices: 7.47 us -> 9.61 us  [per_device(): lax.all_to_all(outgoing_off, 'wide', split_axis=0, concat_axis=0, tiled=T...]
  transfers between devices with their start and end apart: 3 -> 3, of which waited for: 3 -> 3; matrix products, arithmetic and copies ran while one was open for 4% -> 3% of each run, Pallas kernels for 7% -> 7%
where the time goes in v12:
time: 200 us; the launch traced here: 196 us
  waiting for transfers between devices  133 us (66%)
  starting transfers between devices  22.6 us (11%)
  Pallas kernels  20.6 us (10%)
  between operations  13.4 us (7%)
  local copies, waits for them, and re-layouts  4.65 us (2%)
    all_to_all x1, waiting for transfers between devices, per_device(): lax.all_to_all(outgoing_off, 'wide', split_axis=0, concat_axis=0, tiled=T...  86.8 us
    all_gather x1, waiting for transfers between devices, per_device(): shard_blocks = lax.all_gather(prolong, 'narrow', axis=0, tiled=True)  45.4 us
    all_to_all x1, starting transfers between devices, per_device(): lax.all_to_all(outgoing_diag, 'wide', split_axis=0, concat_axis=0, tiled=...  13 us
    pallas_call x2, Pallas kernels, reduce_by_slot(): pl.pallas_call(functools.partial(reduce_kernel, init is not None), out_sh...  10.6 us
    all_to_all x1, starting transfers between devices, per_device(): lax.all_to_all(outgoing_off, 'wide', split_axis=0, concat_axis=0, tiled=T...  9.61 us
    pallas_call x1, Pallas kernels, galerkin_buckets(): pl.pallas_call(functools.partial(galerkin_kernel, n_k), out_shape=jax.Sha...  5.82 us
    pallas_call x1, Pallas kernels, diag_buckets(): pl.pallas_call(diag_kernel, out_shape=jax.ShapeDtypeStruct((owner_count,...  4.18 us
  transfers between devices with their start and end apart: 3, of which 3 were waited for; matrix products, arithmetic and copies ran while one was open for 3% of the time, Pallas kernels for 7%

profile of v12, /device:TPU:7, one launch (start us, length us, event | category | flops | bytes accessed | tf_op | source)
XLA Modules:
  0.0 196.0 jit_solution(12843446094888581260)
XLA Ops:
  6.5 0.0 all-gather.2.cloned.1.call-start
  6.5 0.7 all-gather.2.cloned.1.call-update
  7.3 1.4 copy.24.slot_ref
  8.6 4.2 %shard_map.55 = bf16[32,272,128]{2,1,0:T(8,128)(2,1)} custom-call(s32[16]{0:T(128)} %owner_ref.1, s32[16,3]{1,0:T(8,128)} %copy.24.slot_ref, bf16[16,3,128,128]{3,2,1,0:T(8,128)(2,1)} %refs_1_.1, bf16[16,128,128]{2,1,0:T(8,128)(2,1)} %refs_34_.1), custom_call_target="tpu_custom_call" | custom-call | flops 134217728 | bytes 3276800 | tf_op jit(solution)/shard_map/pallas_call | solution.py:83
  12.8 13.0 %all-to-all-start = ((bf16[32,272,128]{2,1,0:T(8,128)(2,1)}), bf16[32,272,128]{2,1,0:T(8,128)(2,1)S(1)}, u32[]{:S(2)}, u32[]{:S(2)}) async-start(bf16[32,272,128]{2,1,0:T(8,128)(2,1)} %shard_map.55), calls=%async_computation | async-start | bytes 4456448 | tf_op jit(solution)/shard_map/all_to_all | solution.py:208
  25.8 0.0 copy-done.1
  25.8 0.1 copy.29
  25.9 0.0 copy-done
  25.9 0.2 convert_reduce_fusion
  26.1 0.6 add_clamp_fusion.bucket_ref
  26.7 0.6 broadcast_clamp_fusion.cols_ref
  27.3 45.4 %all-gather.2.cloned.1.call-done.refs_2_.refs_3_.refs_4_.refs_5_.refs_6_.refs_7_.refs_8_.refs_9_.refs_10_.refs_11_.refs_12_.refs_13_.refs_14_.refs_15_.refs_16_.refs_17_.refs_18_.refs_19_.refs_20_.refs_21_.refs_22_.refs_23_.refs_24_.refs_25_.refs_26_.refs_27_.refs_28_.refs_29_.refs_30_.refs_31_.refs_32_.refs_33_ = bf16[256,128,128]{2,1,0:T(8,128)(2,1)} async-done(((bf16[16,128,128]{2,1,0:T(8,128)(2,1)}), ...) | async-done | bytes 8388624 | tf_op jit(solution)/shard_map/all_gather | solution.py:214
  72.6 5.8 %shard_map.57 = bf16[64,2,128,128]{3,2,1,0:T(8,128)(2,1)} custom-call(s32[16]{0:T(128)} %add_clamp_fusion.bucket_ref, s32[16,2]{1,0:T(8,128)} %broadcast_clamp_fusion.cols_ref, bf16[16,3,128,128]{3,2,1,0:T(8,128)(2,1)} %refs_1_.1, bf16[16,3,128,128]{3,2,1,0:T(8,128)(2,1)} %refs_1_.1, ...), custom_call_target="tpu_custom_call" | custom-call | flops 268435456 | bytes 6815744 | tf_op jit(solution)/shard_map/pallas_call | solution.py:125
  78.5 0.4 all-to-all-done
  78.9 9.6 %all-to-all-start.1 = ((bf16[32,4,128,128]{3,2,1,0:T(8,128)(2,1)}), bf16[32,4,128,128]{3,2,1,0:T(8,128)(2,1)}, u32[]{:S(2)}, u32[]{:S(2)}) async-start(bf16[32,4,128,128]{3,2,1,0:T(8,128)(2,1)} %bitcast.7), calls=%async_computation.1 | async-start | bytes 8388608 | tf_op jit(solution)/shard_map/all_to_all | solution.py:220
  88.5 0.1 copy.25
  88.6 0.1 copy.27
  88.7 0.6 reshape_squeeze.3.slot_ref
  89.3 0.1 copy.26
  89.4 0.7 reshape.21.slot_ref
  90.1 1.6 slice.23
  91.7 4.5 %shard_map.56.refs_0_ = f32[24,128,128]{2,1,0:T(8,128)} custom-call(s32[64]{0:T(128)} %reshape_squeeze.3.slot_ref, bf16[64,128,128]{2,1,0:T(8,128)(2,1)} %bitcast.8), custom_call_target="tpu_custom_call" | custom-call | flops 1048576 | bytes 5242880 | tf_op jit(solution)/shard_map/pallas_call | solution.py:180
  96.2 86.8 %all-to-all-done.1 = bf16[32,4,128,128]{3,2,1,0:T(8,128)(2,1)} async-done(((bf16[32,4,128,128]{3,2,1,0:T(8,128)(2,1)}), bf16[32,4,128,128]{3,2,1,0:T(8,128)(2,1)}, u32[]{:S(2)}, u32[]{:S(2)}) %all-to-all-start.1) | async-done | bytes 4194336 | tf_op jit(solution)/shard_map/all_to_all | solution.py:220
  183.0 6.1 %shard_map.58 = f32[24,128,128]{2,1,0:T(8,128)} custom-call(s32[128]{0:T(128)} %reshape.21.slot_ref, f32[24,128,128]{2,1,0:T(8,128)} %shard_map.56.refs_0_, bf16[128,128,128]{2,1,0:T(8,128)(2,1)} %bitcast.2.refs_1_), custom_call_target="tpu_custom_call" | custom-call | flops 2097152 | bytes 7340032 | tf_op jit(solution)/shard_map/pallas_call | solution.py:180
  (7 shorter events, 0.0 us)
Async XLA Ops:
  6.5 66.1 %all-gather.2.cloned.1.call-start = ((), (), s32[]{:S(2)}) async-start(), calls=%async_computation.2 | async-start | bytes 8912896 | tf_op jit(solution)/shard_map/all_gather | solution.py:214
  12.8 13.0 %copy-start.1 = (s32[16,3]{0,1:T(4,128)S(1)}, s32[16,3]{0,1:T(4,128)}, u32[]{:S(2)}) copy-start(s32[16,3]{0,1:T(4,128)} %param.6) | copy-start | bytes 580
  12.8 13.1 %copy-start = (s32[16]{0:T(128)S(1)}, s32[16]{0:T(128)}, u32[]{:S(2)}) copy-start(s32[16]{0:T(128)} %owner_ref.1) | copy-start | bytes 196
  12.8 66.1 %all-to-all-start = ((bf16[32,272,128]{2,1,0:T(8,128)(2,1)}), bf16[32,272,128]{2,1,0:T(8,128)(2,1)S(1)}, u32[]{:S(2)}, u32[]{:S(2)}) async-start(bf16[32,272,128]{2,1,0:T(8,128)(2,1)} %shard_map.55), calls=%async_computation | async-start | bytes 4456448 | tf_op jit(solution)/shard_map/all_to_all | solution.py:208
  78.9 104.1 %all-to-all-start.1 = ((bf16[32,4,128,128]{3,2,1,0:T(8,128)(2,1)}), bf16[32,4,128,128]{3,2,1,0:T(8,128)(2,1)}, u32[]{:S(2)}, u32[]{:S(2)}) async-start(bf16[32,4,128,128]{3,2,1,0:T(8,128)(2,1)} %bitcast.7), calls=%async_computation.1 | async-start | bytes 8388608 | tf_op jit(solution)/shard_map/all_to_all | solution.py:220
Sparse Core Ops, SparseCore 0:
  9.4 63.1 all-gather.1

commit v13 on v12

--- a/solution.py
+++ b/solution.py
@@ -18,13 +18,9 @@
     a_refs = refs[:n_k]
     right_refs = refs[n_k:n_k + ROWS_PER_STEP * n_k]
     pt_ref = refs[n_k + ROWS_PER_STEP * n_k]
-    out_ref = refs[n_k + ROWS_PER_STEP * n_k + 1]
+    out_ref, stage_ref, sems = refs[n_k + ROWS_PER_STEP * n_k + 2:]
     step = pl.program_id(0)
-
-    @pl.when(step == 0)
-    def _():
-        out_ref[...] = jnp.zeros_like(out_ref)
-
+    copies = []
     for i in range(ROWS_PER_STEP):
         bucket = bucket_ref[step * ROWS_PER_STEP + i]
         for k in range(n_k):
@@ -34,7 +30,13 @@
             galerkin = lax.dot_general(
                 pt_ref[i], product, (((0,), (0,)), ((), ())), preferred_element_type=jnp.float32
             )
-            out_ref[bucket, k] = galerkin.astype(jnp.bfloat16)
+            slot = i * n_k + k
+            stage_ref[slot] = galerkin.astype(jnp.bfloat16)
+            copy = pltpu.make_async_copy(stage_ref.at[slot], out_ref.at[bucket, k], sems.at[slot])
+            copy.start()
+            copies.append(copy)
+    for copy in copies:
+        copy.wait()
 
 
 META_ROWS = 16
@@ -117,23 +119,27 @@
         for j in range(n_k)
     ]
     pt_spec = pl.BlockSpec((ROWS_PER_STEP, block_size, block_size), lambda s, b, c: (s, 0, 0))
-    out_spec = pl.BlockSpec(
-        (bucket_count, n_k, block_size, block_size), lambda s, b, c: (0, 0, 0, 0)
-    )
+    any_spec = pl.BlockSpec(memory_space=pl.ANY)
     flops = 4 * slab_rows * n_k * block_size ** 3
-    moved = 2 * block_size * block_size * (slab_rows * (2 * n_k + 1) + bucket_count * n_k)
+    moved = 2 * block_size * block_size * slab_rows * (3 * n_k + 1)
+    zeros = jnp.zeros((bucket_count, n_k, block_size, block_size), jnp.bfloat16)
     return pl.pallas_call(
         functools.partial(galerkin_kernel, n_k),
         out_shape=jax.ShapeDtypeStruct((bucket_count, n_k, block_size, block_size), jnp.bfloat16),
         grid_spec=pltpu.PrefetchScalarGridSpec(
             num_scalar_prefetch=2,
             grid=(slab_rows // ROWS_PER_STEP,),
-            in_specs=a_specs + right_specs + [pt_spec],
-            out_specs=out_spec,
-        ),
+            in_specs=a_specs + right_specs + [pt_spec, any_spec],
+            out_specs=any_spec,
+            scratch_shapes=[
+                pltpu.VMEM((ROWS_PER_STEP * n_k, block_size, block_size), jnp.bfloat16),
+                pltpu.SemaphoreType.DMA((ROWS_PER_STEP * n_k,)),
+            ],
+        ),
+        input_output_aliases={2 + n_k + ROWS_PER_STEP * n_k + 1: 0},
         compiler_params=pltpu.CompilerParams(dimension_semantics=("arbitrary",)),
         cost_estimate=pl.CostEstimate(flops=flops, bytes_accessed=moved, transcendentals=0),
-    )(bucket, cols, *([a_blocks] * n_k), *([table] * (ROWS_PER_STEP * n_k)), prolong)
+    )(bucket, cols, *([a_blocks] * n_k), *([table] * (ROWS_PER_STEP * n_k)), prolong, zeros)
 
 
 ACCUMULATORS = 4

time: 200 us -> 201 us (level)
  local copies, waits for them, and re-layouts: 4.65 us -> 7.66 us
    broadcast_in_dim x0 -> x1, local copies, waits for them, and re-layouts: none -> 3.01 us  [galerkin_buckets(): zeros = jnp.zeros((bucket_count, n_k, block_size, block_size), jnp.bfloat16)]
  transfers between devices with their start and end apart: 3 -> 3, of which waited for: 3 -> 2; matrix products, arithmetic and copies ran while one was open for 3% -> 5% of each run, Pallas kernels for 7% -> 7%
where the time goes in v13:
time: 201 us; the launch traced here: 197 us
  waiting for transfers between devices  133 us (66%)
  starting transfers between devices  23 us (11%)
  Pallas kernels  19.1 us (10%)
  between operations  13.5 us (7%)
  local copies, waits for them, and re-layouts  7.66 us (4%)
    all_to_all x1, waiting for transfers between devices, per_device(): lax.all_to_all(outgoing_off, 'wide', split_axis=0, concat_axis=0, tiled=T...  86.8 us
    all_gather x1, waiting for transfers between devices, per_device(): shard_blocks = lax.all_gather(prolong, 'narrow', axis=0, tiled=True)  45.4 us
    all_to_all x1, starting transfers between devices, per_device(): lax.all_to_all(outgoing_diag, 'wide', split_axis=0, concat_axis=0, tiled=...  13 us
    pallas_call x2, Pallas kernels, reduce_by_slot(): pl.pallas_call(functools.partial(reduce_kernel, init is not None), out_sh...  10.6 us
    all_to_all x1, starting transfers between devices, per_device(): lax.all_to_all(outgoing_off, 'wide', split_axis=0, concat_axis=0, tiled=T...  9.99 us
    pallas_call x1, Pallas kernels, galerkin_buckets(): pl.pallas_call(functools.partial(galerkin_kernel, n_k), out_shape=jax.Sha...  4.25 us
    pallas_call x1, Pallas kernels, diag_buckets(): pl.pallas_call(diag_kernel, out_shape=jax.ShapeDtypeStruct((owner_count,...  4.18 us
  transfers between devices with their start and end apart: 3, of which 2 were waited for; matrix products, arithmetic and copies ran while one was open for 5% of the time, Pallas kernels for 7%

profile of v13, /device:TPU:7, one launch (start us, length us, event | category | flops | bytes accessed | tf_op | source)
XLA Modules:
  0.0 197.4 jit_solution(16470247120146243345)
XLA Ops:
  6.5 0.0 all-gather.2.cloned.1.call-start
  6.5 0.7 all-gather.2.cloned.1.call-update
  7.3 1.4 copy.25.slot_ref
  8.6 4.2 %shard_map.55 = bf16[32,272,128]{2,1,0:T(8,128)(2,1)} custom-call(s32[16]{0:T(128)} %owner_ref.1, s32[16,3]{1,0:T(8,128)} %copy.25.slot_ref, bf16[16,3,128,128]{3,2,1,0:T(8,128)(2,1)} %refs_1_.1, bf16[16,128,128]{2,1,0:T(8,128)(2,1)} %refs_34_.1), custom_call_target="tpu_custom_call" | custom-call | flops 134217728 | bytes 3276800 | tf_op jit(solution)/shard_map/pallas_call | solution.py:85
  12.8 13.0 %all-to-all-start = ((bf16[32,272,128]{2,1,0:T(8,128)(2,1)}), bf16[32,272,128]{2,1,0:T(8,128)(2,1)S(1)}, u32[]{:S(2)}, u32[]{:S(2)}) async-start(bf16[32,272,128]{2,1,0:T(8,128)(2,1)} %shard_map.55), calls=%async_computation | async-start | bytes 4456448 | tf_op jit(solution)/shard_map/all_to_all | solution.py:214
  25.8 0.0 copy-done.1
  25.8 0.1 copy.30
  25.9 0.2 convert_reduce_fusion
  26.1 0.6 add_clamp_fusion.bucket_ref
  26.7 0.6 broadcast_clamp_fusion.cols_ref
  27.3 45.4 %all-gather.2.cloned.1.call-done.refs_2_.refs_3_.refs_4_.refs_5_.refs_6_.refs_7_.refs_8_.refs_9_.refs_10_.refs_11_.refs_12_.refs_13_.refs_14_.refs_15_.refs_16_.refs_17_.refs_18_.refs_19_.refs_20_.refs_21_.refs_22_.refs_23_.refs_24_.refs_25_.refs_26_.refs_27_.refs_28_.refs_29_.refs_30_.refs_31_.refs_32_.refs_33_ = bf16[256,128,128]{2,1,0:T(8,128)(2,1)} async-done(((bf16[16,128,128]{2,1,0:T(8,128)(2,1)}), ...) | async-done | bytes 8388624 | tf_op jit(solution)/shard_map/all_gather | solution.py:220
  72.6 3.0 %broadcast_in_dim.2.refs_35_ = bf16[64,2,128,128]{3,2,1,0:T(8,128)(2,1)} broadcast(bf16[]{:T(256)} %constant.12.clone.1), dimensions={} | broadcast | bytes 4194306 | tf_op jit(solution)/shard_map/broadcast_in_dim | solution.py:125
  75.6 4.3 %shard_map.57 = bf16[64,2,128,128]{3,2,1,0:T(8,128)(2,1)} custom-call(s32[16]{0:T(128)} %add_clamp_fusion.bucket_ref, s32[16,2]{1,0:T(8,128)} %broadcast_clamp_fusion.cols_ref, bf16[16,3,128,128]{3,2,1,0:T(8,128)(2,1)} %refs_1_.1, bf16[16,3,128,128]{3,2,1,0:T(8,128)(2,1)} %refs_1_.1, ...), custom_call_target="tpu_custom_call", output_to_operand_aliasing={{}: (37, {})} | custom-call | flops 268435456 | bytes 3670016 | tf_op jit(solution)/shard_map/pallas_call | solution.py:126
  79.9 0.0 all-to-all-done
  79.9 10.0 %all-to-all-start.1 = ((bf16[32,4,128,128]{3,2,1,0:T(8,128)(2,1)}), bf16[32,4,128,128]{3,2,1,0:T(8,128)(2,1)}, u32[]{:S(2)}, u32[]{:S(2)}) async-start(bf16[32,4,128,128]{3,2,1,0:T(8,128)(2,1)} %bitcast.7), calls=%async_computation.1 | async-start | bytes 8388608 | tf_op jit(solution)/shard_map/all_to_all | solution.py:226
  89.9 0.1 copy.26
  90.0 0.1 copy.28
  90.1 0.6 reshape_squeeze.3.slot_ref
  90.8 0.1 copy.27
  90.9 0.7 reshape.21.slot_ref
  91.6 1.6 slice.23
  93.1 4.5 %shard_map.56.refs_0_ = f32[24,128,128]{2,1,0:T(8,128)} custom-call(s32[64]{0:T(128)} %reshape_squeeze.3.slot_ref, bf16[64,128,128]{2,1,0:T(8,128)(2,1)} %bitcast.8), custom_call_target="tpu_custom_call" | custom-call | flops 1048576 | bytes 5242880 | tf_op jit(solution)/shard_map/pallas_call | solution.py:186
  97.7 86.8 %all-to-all-done.1 = bf16[32,4,128,128]{3,2,1,0:T(8,128)(2,1)} async-done(((bf16[32,4,128,128]{3,2,1,0:T(8,128)(2,1)}), bf16[32,4,128,128]{3,2,1,0:T(8,128)(2,1)}, u32[]{:S(2)}, u32[]{:S(2)}) %all-to-all-start.1) | async-done | bytes 4194336 | tf_op jit(solution)/shard_map/all_to_all | solution.py:226
  184.4 6.1 %shard_map.58 = f32[24,128,128]{2,1,0:T(8,128)} custom-call(s32[128]{0:T(128)} %reshape.21.slot_ref, f32[24,128,128]{2,1,0:T(8,128)} %shard_map.56.refs_0_, bf16[128,128,128]{2,1,0:T(8,128)(2,1)} %bitcast.2.refs_1_), custom_call_target="tpu_custom_call" | custom-call | flops 2097152 | bytes 7340032 | tf_op jit(solution)/shard_map/pallas_call | solution.py:186
  (8 shorter events, 0.0 us)
Async XLA Ops:
  6.5 66.1 %all-gather.2.cloned.1.call-start = ((), (), s32[]{:S(2)}) async-start(), calls=%async_computation.2 | async-start | bytes 8912896 | tf_op jit(solution)/shard_map/all_gather | solution.py:220
  12.8 13.0 %copy-start.1 = (s32[16,3]{0,1:T(4,128)S(1)}, s32[16,3]{0,1:T(4,128)}, u32[]{:S(2)}) copy-start(s32[16,3]{0,1:T(4,128)} %param.6) | copy-start | bytes 580
  12.8 13.1 %copy-start = (s32[16]{0:T(128)S(1)}, s32[16]{0:T(128)}, u32[]{:S(2)}) copy-start(s32[16]{0:T(128)} %owner_ref.1) | copy-start | bytes 196
  12.8 67.1 %all-to-all-start = ((bf16[32,272,128]{2,1,0:T(8,128)(2,1)}), bf16[32,272,128]{2,1,0:T(8,128)(2,1)S(1)}, u32[]{:S(2)}, u32[]{:S(2)}) async-start(bf16[32,272,128]{2,1,0:T(8,128)(2,1)} %shard_map.55), calls=%async_computation | async-start | bytes 4456448 | tf_op jit(solution)/shard_map/all_to_all | solution.py:214
  79.9 104.5 %all-to-all-start.1 = ((bf16[32,4,128,128]{3,2,1,0:T(8,128)(2,1)}), bf16[32,4,128,128]{3,2,1,0:T(8,128)(2,1)}, u32[]{:S(2)}, u32[]{:S(2)}) async-start(bf16[32,4,128,128]{3,2,1,0:T(8,128)(2,1)} %bitcast.7), calls=%async_computation.1 | async-start | bytes 8388608 | tf_op jit(solution)/shard_map/all_to_all | solution.py:226
Sparse Core Ops, SparseCore 0:
  9.4 63.1 all-gather.1
